TPU v7x, 32 devices: a whole 2x2x4 slice. The times are simulated.
32 devices in a mesh: seq: 8 (over z, x), tensor: 4 (over y, core).
Axes of the slice: x: 2, y: 2, z: 4, core: 2. Of those that a mesh axis runs over, the one named last changes fastest.
Arguments:
- hidden: bfloat16 [4096, 1280], P(('seq', 'tensor')), may hold values from -6 to 6
- segment_ids: int32 [4096], P('seq'), may hold values from 0 to 3, never falling along the last dimension, each value on 1 to 2048 neighbouring positions
- page_slot: int32 [32], replicated, may hold values from 0 to 31, each once
- in_proj: bfloat16 [1280, 16, 192], P(None, 'tensor'), may hold values from -6 to 6
- out_proj: bfloat16 [1024, 1280], P('tensor'), may hold values from -0.1875 to 0.1875
- up_proj: bfloat16 [1280, 2, 5120], P(None, None, 'tensor'), may hold values from -6 to 6
- down_proj: bfloat16 [5120, 1280], P('tensor'), may hold values from -0.078125 to 0.078125
- score_scale: float32 [16, 64], P('tensor'), may hold values from 0.5 to 2
- mlp_scale: float32 [2, 5120], P(None, 'tensor'), may hold values from 0.5 to 2
- step_rates: float32 [2, 1280], replicated, may hold values from 0.05 to 0.5
Outputs:
- out_state: bfloat16 [4096, 1280], P(('seq', 'tensor'))
- page_cache: bfloat16 [32, 128, 2048], P('seq', None, 'tensor')
Inputs may be any that keep to these rules, and one draw needn't show every extreme that they name: `segment_ids`: never falling along the tokens; each prompt has 1 to 2048 tokens, one exactly 2048. `page_slot`: each slot named by exactly one page.
All inputs are finite; a program needn't handle non-finite values.
Results may differ from a plain program's by a relative error of at most 0.012.
Values may be sent and summed in bfloat16 or wider, within the bound.
No kernel may reach another device: no remote copies, remote signals or barrier semaphores. Data moves between devices by JAX's collectives and lax.ppermute only.
A program may use at most 128 MiB of HBM per device.

v0:
```python
import functools
import math

import jax
import jax.numpy as jnp
from jax import lax
from jax.experimental import pallas as pl
from jax.experimental.pallas import tpu as pltpu
from jax.sharding import PartitionSpec as P

PAGE = 128


EPSILON = 1e-06
NEG_LARGE = -1e30


def unit_rows(matrix):
    return matrix * lax.rsqrt(jnp.sum(matrix * matrix, axis=-1, keepdims=True) + EPSILON)


def gather_rows(part, axis):
    count = lax.axis_size(axis)
    index = lax.axis_index(axis)
    rows = part.shape[0]
    out = jnp.zeros((count * rows, *part.shape[1:]), part.dtype)
    out = lax.dynamic_update_slice_in_dim(out, part, index * rows, 0)
    for shift in range(1, count):
        pairs = [(j, (j + shift) % count) for j in range(count)]
        came = lax.ppermute(part, axis, pairs)
        out = lax.dynamic_update_slice_in_dim(out, came, ((index - shift) % count) * rows, 0)
    return out


def scatter_sum(whole, axis):
    count = lax.axis_size(axis)
    index = lax.axis_index(axis)
    blocks = whole.reshape(count, whole.shape[0] // count, *whole.shape[1:])
    total = lax.dynamic_index_in_dim(blocks, index, 0, keepdims=False).astype(jnp.float32)
    for shift in range(1, count):
        pairs = [(j, (j + shift) % count) for j in range(count)]
        send = lax.dynamic_index_in_dim(blocks, (index + shift) % count, 0, keepdims=False)
        total = total + lax.ppermute(send, axis, pairs).astype(jnp.float32)
    return total


Q_TILE = 512
K_TILE = 256


def attend_kernel(
    bounds_ref, proj_ref, kv_ref, scale_ref, qseg_ref, kseg_ref, out_ref, *, factor, half
):
    rows = qseg_ref.shape[0]
    heads = scale_ref.shape[0]
    lanes = 2 * half
    shard_blocks = (kv_ref.shape[1] - kv_ref.shape[1] % K_TILE) // K_TILE
    tiles = rows // Q_TILE
    first = bounds_ref[2 * tiles]
    fold = factor == 2.0 ** round(math.log2(factor))
    key_lane = lax.broadcasted_iota(jnp.int32, (K_TILE, lanes), 1)
    held = {}
    for head in range(heads):
        scale = scale_ref[head]
        for tile in range(tiles):
            q_raw = proj_ref[tile * Q_TILE : (tile + 1) * Q_TILE, head * lanes : (head + 1) * lanes]
            q_tile = (
                q_raw * lax.rsqrt(jnp.sum(q_raw * q_raw, axis=1, keepdims=True) + EPSILON) * scale
            ).astype(jnp.bfloat16)
            q_seg = qseg_ref[tile * Q_TILE : (tile + 1) * Q_TILE, :]
            q_pos = first + tile * Q_TILE + lax.broadcasted_iota(jnp.int32, (Q_TILE, K_TILE), 0)
            q_norm = jnp.sqrt(
                jnp.sum(jnp.square(q_tile.astype(jnp.float32)), axis=1, keepdims=True)
            )
            shift = factor * q_norm * (jnp.max(scale) * (1.0 + 2.0**-6))
            if fold:
                q_tile = q_tile * jnp.asarray(factor, jnp.bfloat16)

            def step(block, acc, q_tile=q_tile, q_seg=q_seg, q_pos=q_pos, head=head, scale=scale,
                     shift=shift):
                shard = block // shard_blocks
                row_at = pl.multiple_of((block % shard_blocks) * K_TILE, K_TILE)
                key_at = pl.multiple_of(block * K_TILE, K_TILE)
                kv_blk = kv_ref[shard, pl.ds(row_at, K_TILE), head * lanes : (head + 1) * lanes]
                kv_f = kv_blk.astype(jnp.float32)
                k_sq = jnp.where(key_lane < half, kv_f * kv_f, 0.0)
                k_unit = (
                    kv_f * lax.rsqrt(jnp.sum(k_sq, axis=1, keepdims=True) + EPSILON) * scale
                ).astype(jnp.bfloat16)
                k_seg = kseg_ref[:, pl.ds(key_at, K_TILE)]
                scores = lax.dot_general(
                    q_tile, k_unit, (((1,), (1,)), ((), ())), preferred_element_type=jnp.float32
                )
                if not fold:
                    scores = factor * scores
                k_pos = key_at + lax.broadcasted_iota(jnp.int32, (Q_TILE, K_TILE), 1)
                allowed = (q_seg == k_seg) & (k_pos <= q_pos)
                weights = jnp.where(allowed, jnp.exp(scores - shift), 0.0).astype(jnp.bfloat16)
                kv_sum = jnp.where(key_lane == 0, jnp.ones_like(kv_blk), kv_blk)
                return acc + jnp.dot(weights, kv_sum, preferred_element_type=jnp.float32)

            acc = lax.fori_loop(
                bounds_ref[tile],
                bounds_ref[tiles + tile] + 1,
                step,
                jnp.zeros((Q_TILE, lanes), jnp.float32),
            )
            total = acc[:, 0:1]
            result = acc / total
            pair = head // 2
            rows_at = slice(tile * Q_TILE, (tile + 1) * Q_TILE)
            if head % 2 == 0:
                held[tile] = pltpu.roll(result, half, 1)
                if head == heads - 1:
                    out_ref[rows_at, pair * lanes : (pair + 1) * lanes] = held[tile].astype(
                        out_ref.dtype
                    )
            else:
                joined = jnp.where(
                    lax.broadcasted_iota(jnp.int32, (Q_TILE, lanes), 1) < half, held[tile], result
                )
                out_ref[rows_at, pair * lanes : (pair + 1) * lanes] = joined.astype(out_ref.dtype)


def flash_attend(bounds, proj, gathered, scale_pad, query_segs, key_segs, factor, half):
    rows = query_segs.shape[0]
    heads, _, lanes = scale_pad.shape
    keys = key_segs.shape[1]
    vmem = pl.BlockSpec(memory_space=pltpu.VMEM)
    return pl.pallas_call(
        functools.partial(attend_kernel, factor=factor, half=half),
        out_shape=jax.ShapeDtypeStruct((rows, -(-heads // 2) * lanes), jnp.bfloat16),
        in_specs=[pl.BlockSpec(memory_space=pltpu.SMEM)] + [vmem] * 5,
        out_specs=vmem,
        cost_estimate=pl.CostEstimate(
            flops=4 * heads * rows * keys * lanes,
            transcendentals=heads * rows * keys,
            bytes_accessed=heads * keys * lanes * 2,
        ),
    )(bounds, proj, gathered, scale_pad, query_segs, key_segs)


def body(
    hidden,
    segment_ids,
    page_slot,
    in_proj,
    out_proj,
    up_proj,
    down_proj,
    score_scale,
    mlp_scale,
    step_rates,
):
    seq_count = lax.axis_size("seq")
    seq_index = lax.axis_index("seq")
    local_tokens = segment_ids.shape[0]
    heads_dev, head_dim = score_scale.shape
    model_width = hidden.shape[1]
    hidden_dev = down_proj.shape[0]
    pages_dev = local_tokens // PAGE
    channels = heads_dev * 2 * head_dim
    state_own = unit_rows(hidden.astype(jnp.float32)).astype(jnp.bfloat16)
    gathered_state = gather_rows(state_own, "tensor")
    lanes = 2 * head_dim
    projected = jnp.dot(
        gathered_state,
        in_proj.reshape(model_width, heads_dev * 3 * head_dim),
        preferred_element_type=jnp.float32,
    )
    width = 3 * head_dim
    query_pad = jnp.concatenate(
        sum(
            [
                [
                    projected[:, h * width : h * width + head_dim],
                    jnp.zeros((local_tokens, head_dim), jnp.float32),
                ]
                for h in range(heads_dev)
            ],
            [],
        ),
        axis=1,
    )
    key_value = jnp.concatenate(
        [projected[:, h * width + head_dim : (h + 1) * width] for h in range(heads_dev)], axis=1
    ).astype(jnp.bfloat16)
    first_token = seq_index * local_tokens
    seg_rows = -(-local_tokens // channels)
    seg_flat = jnp.pad(segment_ids, (0, seg_rows * channels - local_tokens))
    kv_ext = jnp.concatenate(
        [key_value, seg_flat.astype(jnp.bfloat16).reshape(seg_rows, channels)], axis=0
    )
    gathered = lax.all_gather(kv_ext, "seq", axis=0, tiled=False)
    seg_piece = (
        gathered[:, local_tokens:].reshape(seq_count, seg_rows * channels)[:, :local_tokens]
        .reshape(-1)
        .astype(jnp.int32)
    )
    piece_rows = seq_count * local_tokens
    scale_pad = jnp.pad(score_scale, ((0, 0), (0, lanes - head_dim))).reshape(heads_dev, 1, lanes)
    tiles = local_tokens // Q_TILE
    tile_first = first_token + Q_TILE * jnp.arange(tiles, dtype=jnp.int32)
    tile_seg = segment_ids.reshape(tiles, Q_TILE)[:, 0]
    block_last_seg = seg_piece.reshape(piece_rows // K_TILE, K_TILE)[:, -1]
    block_lo = jnp.sum(
        (block_last_seg[None, :] < tile_seg[:, None]).astype(jnp.int32), axis=1
    )
    block_hi = (tile_first + Q_TILE - 1) // K_TILE
    bounds = jnp.concatenate([block_lo, block_hi, first_token[None]]).astype(jnp.int32)
    heads_pad = flash_attend(
        bounds,
        query_pad,
        gathered,
        scale_pad,
        segment_ids.reshape(local_tokens, 1),
        seg_piece.reshape(1, piece_rows),
        math.sqrt(head_dim),
        head_dim,
    )
    heads_flat = heads_pad[:, : heads_dev * head_dim]
    slots_dev = page_slot.shape[0] // seq_count
    my_slots = seq_index * slots_dev + jnp.arange(slots_dev, dtype=jnp.int32)
    page_ids = jnp.arange(page_slot.shape[0], dtype=jnp.int32)
    source_page = jnp.sum(
        jnp.where(page_slot[None, :] == my_slots[:, None], page_ids[None, :], 0), axis=1
    )
    page_cache = jnp.stack(
        [
            lax.dynamic_slice(
                gathered,
                (source_page[j] // pages_dev, (source_page[j] % pages_dev) * PAGE, 0),
                (1, PAGE, channels),
            )[0]
            for j in range(slots_dev)
        ]
    )
    chosen = heads_flat
    attn_own = scatter_sum(
        jnp.dot(chosen, out_proj, preferred_element_type=jnp.float32).astype(jnp.bfloat16),
        "tensor",
    )
    state_f = state_own.astype(jnp.float32)
    middle = unit_rows(state_f + step_rates[0] * (unit_rows(attn_own) - state_f))
    mid_rows = gather_rows(middle.astype(jnp.bfloat16), "tensor")
    both = jnp.einsum("td,dkf->tkf", mid_rows, up_proj, preferred_element_type=jnp.float32)
    act = (
        both[:, 0] * mlp_scale[0] * jax.nn.silu(both[:, 1] * mlp_scale[1] * math.sqrt(model_width))
    ).astype(jnp.bfloat16)
    chosen = act
    mlp_own = scatter_sum(
        jnp.dot(chosen, down_proj, preferred_element_type=jnp.float32).astype(jnp.bfloat16),
        "tensor",
    )
    final = unit_rows(middle + step_rates[1] * (unit_rows(mlp_own) - middle))
    out_state = (math.sqrt(model_width) * final).astype(jnp.bfloat16)
    return (out_state, page_cache)


def solution(mesh):
    return jax.shard_map(
        body,
        mesh=mesh,
        in_specs=(
            P(("seq", "tensor"), None),
            P("seq"),
            P(),
            P(None, "tensor", None),
            P("tensor", None),
            P(None, None, "tensor"),
            P("tensor", None),
            P("tensor", None),
            P(None, "tensor"),
            P(),
        ),
        out_specs=(P(("seq", "tensor"), None), P("seq", None, "tensor")),
        check_vma=False,
    )
```

profile of v0, /device:TPU:24, one launch (start us, length us, event | category | flops | bytes accessed | tf_op | source)
XLA Modules:
  0.0 216.5 jit_solution(8304773382590320536)
XLA Ops:
  7.2 0.0 copy-start
  7.2 0.0 all-gather.4.cloned.1.call-start
  7.2 1.3 fusion.9
  8.5 1.2 broadcast.73.clone
  9.7 1.0 constant_dynamic-update-slice_fusion.7
  10.7 1.5 collective-permute-start.1
  12.2 1.4 collective-permute-start.2
  13.7 6.8 %collective-permute-done = bf16[128,1280]{1,0:T(8,128)(2,1)} collective-permute-done((bf16[128,1280]{1,0:T(8,128)(2,1)}, bf16[128,1280]{1,0:T(8,128)(2,1)}, u32[]{:S(2)}, u32[]{:S(2)}) %collective-permute-start) | collective-permute-done | bytes 327712 | tf_op jit(solution)/shard_map/ppermute | solution.py:30
  20.4 1.7 constant_dynamic-update-slice_fusion.6
  22.2 1.7 constant_dynamic-update-slice_fusion.5
  23.9 3.2 %collective-permute-done.2 = bf16[128,1280]{1,0:T(8,128)(2,1)} collective-permute-done((bf16[128,1280]{1,0:T(8,128)(2,1)}, bf16[128,1280]{1,0:T(8,128)(2,1)}, u32[]{:S(2)}, u32[]{:S(2)}) %collective-permute-start.2) | collective-permute-done | bytes 327712 | tf_op jit(solution)/shard_map/ppermute | solution.py:30
  27.0 1.7 constant_dynamic-update-slice_fusion.4
  28.8 3.7 %fusion.23 = (bf16[512,768]{1,0:T(8,128)(2,1)S(1)}, f32[512,768]{1,0:T(8,128)}) fusion(bf16[512,1280]{1,0:T(8,128)(2,1)} %constant_dynamic-update-slice_fusion.4, bf16[1280,768]{0,1:T(8,128)(2,1)S(1)} %bitcast.81), kind=kOutput, calls=%fused_computation.73 | convolution fusion | flops 1007026176 | bytes 5636096 | tf_op jit(solution)/shard_map/dot_general | solution.py:166
  32.5 0.1 fusion.21
  32.6 0.9 maximum_bitcast_fusion
  33.5 0.0 all-gather.4.cloned.1.call-update
  33.6 0.6 slice.102
  34.2 0.9 copy.17.qseg_ref
  35.0 0.6 pad.4
  35.6 2.3 %fusion.20 = (f32[512,64]{1,0:T(8,128)}, f32[512,64]{1,0:T(8,128)}, f32[512,64]{1,0:T(8,128)}, f32[512,64]{1,0:T(8,128)}) fusion(f32[512,768]{1,0:T(8,128)} %get-tuple-element.39), kind=kLoop, calls=%fused_computation.70 | loop fusion | bytes 1048576 | tf_op jit(solution)/shard_map/slice | solution.py:176
  37.9 2.3 %concatenate.16.proj_ref = f32[512,512]{1,0:T(8,128)} concatenate(f32[512,64]{1,0:T(8,128)} %get-tuple-element.23, f32[512,64]{1,0:T(8,128)S(1)} %broadcast.74, f32[512,64]{1,0:T(8,128)} %get-tuple-element.22, f32[512,64]{1,0:T(8,128)S(1)} %broadcast.74, f32[512,64]{1,0:T(8,128)} %get-tuple-element.21, f32[512,64]{1,0:T(8,128)S(1)} %broadcast.74, f32[512,64]{1,0:T(8,128)} %get-tuple-element.20, ...), dimensions={1} | concatenate | bytes 2097152 | tf_op jit(solution)/shard_map/concatenate | solution.py:172
  40.3 68.4 %all-gather.4.cloned.1.call-done.kv_ref = bf16[8,513,512]{2,1,0:T(8,128)(2,1)} async-done(((bf16[1,513,512]{2,1,0:T(8,128)(2,1)}), bf16[8,513,512]{2,1,0:T(8,128)(2,1)}) %all-gather.4.cloned.1.call-update) | async-done | bytes 4202512 | tf_op jit(solution)/shard_map/all_gather | solution.py:194
  108.7 0.9 fusion.19
  109.6 0.6 convert.16.kseg_ref
  110.2 1.4 convert_reduce_fusion
  111.6 1.2 pad_add_fusion.bounds_ref
  112.8 24.6 %shard_map.113 = bf16[512,256]{1,0:T(8,128)(2,1)} custom-call(s32[3]{0:T(128)} %pad_add_fusion.bounds_ref, f32[512,512]{1,0:T(8,128)} %concatenate.16.proj_ref, bf16[8,513,512]{2,1,0:T(8,128)(2,1)} %all-gather.4.cloned.1.call-done.kv_ref, f32[4,1,128]{2,1,0:T(1,128)} %bitcast.80, s32[512,1]{1,0:T(8,128)} %copy.17.qseg_ref, s32[1,4096]{1,0:T(1,128)} %convert.16.kseg_ref), custom_call_target="tpu_custom_call" | custom-call | flops 4294967296 | bytes 4194304 | tf_op jit(solution)/shard_map/pallas_call | solution.py:130
  137.4 1.7 convolution_convert_fusion.1
  139.1 0.0 copy-start.7
  139.1 1.1 copy-done.1
  140.2 1.0 dynamic-slice_bitcast_fusion.5
  141.2 0.0 collective-permute-start.3
  141.2 1.5 collective-permute-start.4
  142.7 1.4 collective-permute-start.5
  144.2 6.8 %collective-permute-done.3 = bf16[128,1280]{1,0:T(8,128)(2,1)} collective-permute-done((bf16[128,1280]{1,0:T(8,128)(2,1)}, bf16[128,1280]{1,0:T(8,128)(2,1)}, u32[]{:S(2)}, u32[]{:S(2)}) %collective-permute-start.3) | collective-permute-done | bytes 327712 | tf_op jit(solution)/shard_map/ppermute | solution.py:43
  151.0 1.1 collective-permute-done.4
  152.1 5.5 %collective-permute-done.5 = bf16[128,1280]{1,0:T(8,128)(2,1)} collective-permute-done((bf16[128,1280]{1,0:T(8,128)(2,1)}, bf16[128,1280]{1,0:T(8,128)(2,1)}, u32[]{:S(2)}, u32[]{:S(2)}) %collective-permute-start.5) | collective-permute-done | bytes 327712 | tf_op jit(solution)/shard_map/ppermute | solution.py:43
  157.5 1.5 multiply_reduce_fusion.3
  159.1 1.8 multiply_reduce_fusion.2
  160.9 0.0 copy-start.12
  160.9 0.1 broadcast.73
  161.0 0.1 constant_dynamic-update-slice_fusion.3
  161.1 0.6 copy-done.2
  161.7 0.8 collective-permute-start.6
  162.5 0.2 select_reduce_fusion
  162.7 1.5 collective-permute-start.7
  164.3 0.2 collective-permute-start.8
  164.5 5.8 %collective-permute-done.6 = bf16[128,1280]{1,0:T(8,128)(2,1)S(1)} collective-permute-done((bf16[128,1280]{1,0:T(8,128)(2,1)S(1)}, bf16[128,1280]{1,0:T(8,128)(2,1)S(1)}, u32[]{:S(2)}, u32[]{:S(2)}) %collective-permute-start.6) | collective-permute-done | bytes 327712 | tf_op jit(solution)/shard_map/ppermute | solution.py:30
  170.4 3.1 %collective-permute-done.7 = bf16[128,1280]{1,0:T(8,128)(2,1)S(1)} collective-permute-done((bf16[128,1280]{1,0:T(8,128)(2,1)S(1)}, bf16[128,1280]{1,0:T(8,128)(2,1)S(1)}, u32[]{:S(2)}, u32[]{:S(2)}) %collective-permute-start.7) | collective-permute-done | bytes 327712 | tf_op jit(solution)/shard_map/ppermute | solution.py:30
  173.5 3.5 %collective-permute-done.8 = bf16[128,1280]{1,0:T(8,128)(2,1)S(1)} collective-permute-done((bf16[128,1280]{1,0:T(8,128)(2,1)S(1)}, bf16[128,1280]{1,0:T(8,128)(2,1)S(1)}, u32[]{:S(2)}, u32[]{:S(2)}) %collective-permute-start.8) | collective-permute-done | bytes 327712 | tf_op jit(solution)/shard_map/ppermute | solution.py:30
  177.0 6.4 %fusion = f32[512,2,1280]{2,0,1:T(8,128)S(1)} fusion(bf16[1280,2,1280]{2,1,0:T(2,128)(2,1)} %param.15, bf16[512,1280]{1,0:T(8,128)(2,1)S(1)} %constant_dynamic-update-slice_fusion), kind=kOutput, calls=%fused_computation | convolution fusion | flops 3355443200 | bytes 13107200 | tf_op jit(solution)/shard_map/td,dkf->tkf/dot_general | solution.py:246
  183.4 2.4 %convolution_convert_fusion = bf16[512,1280]{1,0:T(8,128)(2,1)S(1)} fusion(bf16[1280,1280]{1,0:T(8,128)(2,1)S(1)} %copy-done, f32[512,2,1280]{2,0,1:T(8,128)S(1)} %fusion, f32[1280]{0:T(1024)S(1)} %get-tuple-element.5, f32[1280]{0:T(1024)S(1)} %get-tuple-element.4), kind=kOutput, calls=%fused_computation.2 | convolution fusion | flops 1684275200 | bytes 9840640 | tf_op jit(solution)/shard_map/dot_general | solution.py:252
  185.8 1.1 copy-done.4
  186.9 1.0 dynamic-slice_bitcast_fusion.2
  187.9 1.5 collective-permute-start.10
  189.3 1.6 collective-permute-start.11
  191.0 0.7 fusion.22
  201.8 1.4 constant_dynamic-slice_fusion.3
  203.1 0.9 pad_maximum_fusion
  204.0 0.6 collective-permute-done.11
  204.6 1.1 collective-permute-done.9
  205.8 1.4 multiply_reduce_fusion.1
  207.3 1.6 multiply_reduce_fusion
  208.8 0.9 multiply_convert_fusion
  (39 shorter events, 0.3 us)
Async XLA Ops:
  7.2 176.2 %copy-start = (bf16[1280,1280]{1,0:T(8,128)(2,1)S(1)}, bf16[1280,1280]{1,0:T(8,128)(2,1)}, u32[]{:S(2)}) copy-start(bf16[1280,1280]{1,0:T(8,128)(2,1)} %param.16) | copy-start | bytes 9830404
  7.2 101.5 %all-gather.4.cloned.1.call-start = ((), (), s32[]{:S(2)}) async-start(), calls=%async_computation | async-start | bytes 4792320 | tf_op jit(solution)/shard_map/all_gather | solution.py:194
  7.2 6.4 %copy-start.9 = (s32[512]{0:T(512)S(1)}, s32[512]{0:T(512)}, u32[]{:S(2)}) copy-start(s32[512]{0:T(512)} %param.11) | copy-start | bytes 6148
  8.5 1.2 copy-start.6
  10.7 9.8 %collective-permute-start = (bf16[128,1280]{1,0:T(8,128)(2,1)}, bf16[128,1280]{1,0:T(8,128)(2,1)}, u32[]{:S(2)}, u32[]{:S(2)}) collective-permute-start(bf16[128,1280]{1,0:T(8,128)(2,1)} %get-tuple-element.13), channel_id=1, source_target_pairs={{0,1},{1,2},{2,3},{3,0},{4,5},{5,6},{6,7},{7,4},{8,9},{9,10},{10,1... | collective-permute-start | bytes 983048 | tf_op jit(solution)/shard_map/ppermute | solution.py:30
  10.7 11.5 %collective-permute-start.1 = (bf16[128,1280]{1,0:T(8,128)(2,1)}, bf16[128,1280]{1,0:T(8,128)(2,1)}, u32[]{:S(2)}, u32[]{:S(2)}) collective-permute-start(bf16[128,1280]{1,0:T(8,128)(2,1)} %get-tuple-element.13), channel_id=1, source_target_pairs={{0,2},{1,3},{2,0},{3,1},{4,6},{5,7},{6,4},{7,5},{8,10},{9,11},{10,... | collective-permute-start | bytes 983048 | tf_op jit(solution)/shard_map/ppermute | solution.py:30
  12.2 14.8 %collective-permute-start.2 = (bf16[128,1280]{1,0:T(8,128)(2,1)}, bf16[128,1280]{1,0:T(8,128)(2,1)}, u32[]{:S(2)}, u32[]{:S(2)}) collective-permute-start(bf16[128,1280]{1,0:T(8,128)(2,1)} %get-tuple-element.13), channel_id=1, source_target_pairs={{0,3},{1,0},{2,1},{3,2},{4,7},{5,4},{6,5},{7,6},{8,11},{9,8},{10,9... | collective-permute-start | bytes 983048 | tf_op jit(solution)/shard_map/ppermute | solution.py:30
  13.7 15.1 %copy-start.11 = (bf16[1280,4,192]{0,2,1:T(8,128)(2,1)S(1)}, bf16[1280,4,192]{0,2,1:T(8,128)(2,1)}, u32[]{:S(2)}) copy-start(bf16[1280,4,192]{0,2,1:T(8,128)(2,1)} %param.13) | copy-start | bytes 5898244
  32.5 2.5 %copy-start.10 = (f32[4,64]{1,0:T(4,128)S(1)}, f32[4,64]{1,0:T(4,128)}, u32[]{:S(2)}) copy-start(f32[4,64]{1,0:T(4,128)} %param.17) | copy-start | bytes 3076
  139.1 1.1 copy-start.1
  139.1 5.0 %copy-start.7 = (f32[2,1280]{1,0:T(2,128)S(1)}, f32[2,1280]{1,0:T(2,128)}, u32[]{:S(2)}) copy-start(f32[2,1280]{1,0:T(2,128)} %param.19) | copy-start | bytes 30724
  141.2 9.8 %collective-permute-start.3 = (bf16[128,1280]{1,0:T(8,128)(2,1)}, bf16[128,1280]{1,0:T(8,128)(2,1)}, u32[]{:S(2)}, u32[]{:S(2)}) collective-permute-start(bf16[128,1280]{1,0:T(8,128)(2,1)} %get-tuple-element.27), channel_id=1, source_target_pairs={{0,1},{1,2},{2,3},{3,0},{4,5},{5,6},{6,7},{7,4},{8,9},{9,10},{10,1... | collective-permute-start | bytes 983048 | tf_op jit(solution)/shard_map/ppermute | solution.py:43
  141.2 10.9 %collective-permute-start.4 = (bf16[128,1280]{1,0:T(8,128)(2,1)}, bf16[128,1280]{1,0:T(8,128)(2,1)}, u32[]{:S(2)}, u32[]{:S(2)}) collective-permute-start(bf16[128,1280]{1,0:T(8,128)(2,1)} %get-tuple-element.29), channel_id=1, source_target_pairs={{0,2},{1,3},{2,0},{3,1},{4,6},{5,7},{6,4},{7,5},{8,10},{9,11},{10,... | collective-permute-start | bytes 983048 | tf_op jit(solution)/shard_map/ppermute | solution.py:43
  142.7 14.8 %collective-permute-start.5 = (bf16[128,1280]{1,0:T(8,128)(2,1)}, bf16[128,1280]{1,0:T(8,128)(2,1)}, u32[]{:S(2)}, u32[]{:S(2)}) collective-permute-start(bf16[128,1280]{1,0:T(8,128)(2,1)} %get-tuple-element.28), channel_id=1, source_target_pairs={{0,3},{1,0},{2,1},{3,2},{4,7},{5,4},{6,5},{7,6},{8,11},{9,8},{10,9... | collective-permute-start | bytes 983048 | tf_op jit(solution)/shard_map/ppermute | solution.py:43
  160.9 0.8 copy-start.2
  160.9 1.7 copy-start.12
  160.9 3.4 %copy-start.8 = (f32[2,1280]{1,0:T(2,128)S(1)}, f32[2,1280]{1,0:T(2,128)}, u32[]{:S(2)}) copy-start(f32[2,1280]{1,0:T(2,128)} %param.18) | copy-start | bytes 30724
  161.7 8.6 %collective-permute-start.6 = (bf16[128,1280]{1,0:T(8,128)(2,1)S(1)}, bf16[128,1280]{1,0:T(8,128)(2,1)S(1)}, u32[]{:S(2)}, u32[]{:S(2)}) collective-permute-start(bf16[128,1280]{1,0:T(8,128)(2,1)S(1)} %get-tuple-element.9), channel_id=1, source_target_pairs={{0,1},{1,2},{2,3},{3,0},{4,5},{5,6},{6,7},{7,4},{8,9},{9,10},{10,1... | collective-permute-start | bytes 983048 | tf_op jit(solution)/shard_map/ppermute | solution.py:30
  162.7 10.7 %collective-permute-start.7 = (bf16[128,1280]{1,0:T(8,128)(2,1)S(1)}, bf16[128,1280]{1,0:T(8,128)(2,1)S(1)}, u32[]{:S(2)}, u32[]{:S(2)}) collective-permute-start(bf16[128,1280]{1,0:T(8,128)(2,1)S(1)} %get-tuple-element.9), channel_id=1, source_target_pairs={{0,2},{1,3},{2,0},{3,1},{4,6},{5,7},{6,4},{7,5},{8,10},{9,11},{10,... | collective-permute-start | bytes 983048 | tf_op jit(solution)/shard_map/ppermute | solution.py:30
  164.3 12.7 %collective-permute-start.8 = (bf16[128,1280]{1,0:T(8,128)(2,1)S(1)}, bf16[128,1280]{1,0:T(8,128)(2,1)S(1)}, u32[]{:S(2)}, u32[]{:S(2)}) collective-permute-start(bf16[128,1280]{1,0:T(8,128)(2,1)S(1)} %get-tuple-element.9), channel_id=1, source_target_pairs={{0,3},{1,0},{2,1},{3,2},{4,7},{5,4},{6,5},{7,6},{8,11},{9,8},{10,9... | collective-permute-start | bytes 983048 | tf_op jit(solution)/shard_map/ppermute | solution.py:30
  185.8 1.1 copy-start.4
  187.9 16.1 %collective-permute-start.10 = (bf16[128,1280]{1,0:T(8,128)(2,1)}, bf16[128,1280]{1,0:T(8,128)(2,1)}, u32[]{:S(2)}, u32[]{:S(2)}) collective-permute-start(bf16[128,1280]{1,0:T(8,128)(2,1)} %get-tuple-element.26), channel_id=1, source_target_pairs={{0,2},{1,3},{2,0},{3,1},{4,6},{5,7},{6,4},{7,5},{8,10},{9,11},{10,... | collective-permute-start | bytes 983048 | tf_op jit(solution)/shard_map/ppermute | solution.py:43
  189.3 15.3 %collective-permute-start.11 = (bf16[128,1280]{1,0:T(8,128)(2,1)}, bf16[128,1280]{1,0:T(8,128)(2,1)}, u32[]{:S(2)}, u32[]{:S(2)}) collective-permute-start(bf16[128,1280]{1,0:T(8,128)(2,1)} %get-tuple-element.25), channel_id=1, source_target_pairs={{0,3},{1,0},{2,1},{3,2},{4,7},{5,4},{6,5},{7,6},{8,11},{9,8},{10,9... | collective-permute-start | bytes 983048 | tf_op jit(solution)/shard_map/ppermute | solution.py:43
  191.0 14.8 %collective-permute-start.9 = (bf16[128,1280]{1,0:T(8,128)(2,1)}, bf16[128,1280]{1,0:T(8,128)(2,1)}, u32[]{:S(2)}, u32[]{:S(2)}) collective-permute-start(bf16[128,1280]{1,0:T(8,128)(2,1)} %get-tuple-element.24), channel_id=1, source_target_pairs={{0,1},{1,2},{2,3},{3,0},{4,5},{5,6},{6,7},{7,4},{8,9},{9,10},{10,1... | collective-permute-start | bytes 983048 | tf_op jit(solution)/shard_map/ppermute | solution.py:43
  201.8 4.0 %copy-start.5 = (bf16[512,1280]{1,0:T(8,128)(2,1)S(1)}, bf16[512,1280]{1,0:T(8,128)(2,1)}, u32[]{:S(2)}) copy-start(bf16[512,1280]{1,0:T(8,128)(2,1)} %copy-done.4) | copy-start | bytes 3932164
  203.1 4.1 %copy-start.3 = (f32[128,1280]{1,0:T(8,128)S(1)}, f32[128,1280]{1,0:T(8,128)}, u32[]{:S(2)}) copy-start(f32[128,1280]{1,0:T(8,128)} %copy-done.2) | copy-start | bytes 1966084
Sparse Core Ops, SparseCore 0:
  33.6 74.9 all-gather.3
where the time goes:
time: 216 us; the launch traced here: 217 us
  waiting for transfers between devices  106 us (49%)
  Pallas kernels  24.6 us (11%)
  between operations  24.4 us (11%)
  local copies, waits for them, and re-layouts  21 us (10%)
  other arithmetic  14.7 us (7%)
  matrix products  14.2 us (7%)
  starting transfers between devices  11.7 us (5%)
    all_gather x1, waiting for transfers between devices, body(): gathered = lax.all_gather(kv_ext, 'seq', axis=0, tiled=False)  68.4 us
    pallas_call x1, Pallas kernels, flash_attend(): pl.pallas_call(functools.partial(attend_kernel, factor=factor, half=half)...  24.6 us
    ppermute x6, waiting for transfers between devices, gather_rows(): came = lax.ppermute(part, axis, pairs)  22.3 us
    ppermute x6, waiting for transfers between devices, scatter_sum(): total = total + lax.ppermute(send, axis, pairs).astype(jnp.float32)  15.1 us
    reduce_sum x5, other arithmetic, unit_rows(): jnp.sum(matrix * matrix, axis=-1, keepdims=True) + EPSILON  7.59 us
    dot_general x1, matrix products, body(): jnp.einsum('td,dkf->tkf', mid_rows, up_proj, preferred_element_type=jnp.f...  6.36 us
    ppermute x6, starting transfers between devices, scatter_sum(): total = total + lax.ppermute(send, axis, pairs).astype(jnp.float32)  6.06 us
    ppermute x6, starting transfers between devices, gather_rows(): came = lax.ppermute(part, axis, pairs)  5.56 us
  transfers between devices with their start and end apart: 13, of which 11 were waited for; matrix products, arithmetic and copies ran while one was open for 6% of the time, Pallas kernels for 0%

commit v1 on v0

--- a/solution.py
+++ b/solution.py
@@ -45,7 +45,7 @@
 
 
 Q_TILE = 512
-K_TILE = 256
+K_TILE = 512
 
 
 def attend_kernel(

time: 216 us -> 210 us (0.972)
  the two profiles are of different devices: /device:TPU:24 before, /device:TPU:10 now
where the time goes in v1:
time: 210 us; the launch traced here: 208 us
  waiting for transfers between devices  106 us (50%)
  between operations  24.7 us (12%)
  local copies, waits for them, and re-layouts  21.6 us (10%)
  Pallas kernels  15.9 us (8%)
  matrix products  14.2 us (7%)
  other arithmetic  14 us (7%)
  starting transfers between devices  11.7 us (6%)
    all_gather x1, waiting for transfers between devices, body(): gathered = lax.all_gather(kv_ext, 'seq', axis=0, tiled=False)  68.7 us
    ppermute x6, waiting for transfers between devices, gather_rows(): came = lax.ppermute(part, axis, pairs)  22.3 us
    pallas_call x1, Pallas kernels, flash_attend(): pl.pallas_call(functools.partial(attend_kernel, factor=factor, half=half)...  15.9 us
    ppermute x6, waiting for transfers between devices, scatter_sum(): total = total + lax.ppermute(send, axis, pairs).astype(jnp.float32)  14.9 us
    reduce_sum x5, other arithmetic, unit_rows(): jnp.sum(matrix * matrix, axis=-1, keepdims=True) + EPSILON  7.59 us
    dot_general x1, matrix products, body(): jnp.einsum('td,dkf->tkf', mid_rows, up_proj, preferred_element_type=jnp.f...  6.36 us
    ppermute x6, starting transfers between devices, scatter_sum(): total = total + lax.ppermute(send, axis, pairs).astype(jnp.float32)  6.06 us
    ppermute x6, starting transfers between devices, gather_rows(): came = lax.ppermute(part, axis, pairs)  5.59 us
  transfers between devices with their start and end apart: 13, of which 11 were waited for; matrix products, arithmetic and copies ran while one was open for 6% of the time, Pallas kernels for 0%

profile of v1, /device:TPU:10, one launch (start us, length us, event | category | flops | bytes accessed | tf_op | source)
XLA Modules:
  0.0 208.0 jit_solution(4672603805231779259)
XLA Ops:
  7.2 0.0 copy-start
  7.2 0.0 all-gather.4.cloned.1.call-start
  7.2 1.3 fusion.9
  8.5 1.2 broadcast.73.clone
  9.7 0.9 constant_dynamic-update-slice_fusion.7
  10.7 1.6 collective-permute-start.1
  12.2 1.4 collective-permute-start.2
  13.7 0.0 copy-start.11
  13.7 6.7 %collective-permute-done = bf16[128,1280]{1,0:T(8,128)(2,1)} collective-permute-done((bf16[128,1280]{1,0:T(8,128)(2,1)}, bf16[128,1280]{1,0:T(8,128)(2,1)}, u32[]{:S(2)}, u32[]{:S(2)}) %collective-permute-start) | collective-permute-done | bytes 327712 | tf_op jit(solution)/shard_map/ppermute | solution.py:30
  20.4 1.7 constant_dynamic-update-slice_fusion.6
  22.1 1.7 constant_dynamic-update-slice_fusion.5
  23.9 3.2 %collective-permute-done.2 = bf16[128,1280]{1,0:T(8,128)(2,1)} collective-permute-done((bf16[128,1280]{1,0:T(8,128)(2,1)}, bf16[128,1280]{1,0:T(8,128)(2,1)}, u32[]{:S(2)}, u32[]{:S(2)}) %collective-permute-start.2) | collective-permute-done | bytes 327712 | tf_op jit(solution)/shard_map/ppermute | solution.py:30
  27.0 1.7 constant_dynamic-update-slice_fusion.4
  28.8 3.7 %fusion.22 = (bf16[512,768]{1,0:T(8,128)(2,1)S(1)}, f32[512,768]{1,0:T(8,128)}) fusion(bf16[512,1280]{1,0:T(8,128)(2,1)} %constant_dynamic-update-slice_fusion.4, bf16[1280,768]{0,1:T(8,128)(2,1)S(1)} %bitcast.85), kind=kOutput, calls=%fused_computation.73 | convolution fusion | flops 1007026176 | bytes 5636096 | tf_op jit(solution)/shard_map/dot_general | solution.py:166
  32.5 0.1 fusion.20
  32.6 0.9 maximum_bitcast_fusion
  33.5 0.0 all-gather.4.cloned.1.call-update
  33.6 0.6 slice.102
  34.1 0.9 copy.19.qseg_ref
  35.0 0.6 pad.4
  35.6 2.3 %fusion.19 = (f32[512,64]{1,0:T(8,128)}, f32[512,64]{1,0:T(8,128)}, f32[512,64]{1,0:T(8,128)}, f32[512,64]{1,0:T(8,128)}) fusion(f32[512,768]{1,0:T(8,128)} %get-tuple-element.39), kind=kLoop, calls=%fused_computation.70 | loop fusion | bytes 1048576 | tf_op jit(solution)/shard_map/slice | solution.py:176
  37.9 2.3 %concatenate.16.proj_ref = f32[512,512]{1,0:T(8,128)} concatenate(f32[512,64]{1,0:T(8,128)} %get-tuple-element.21, f32[512,64]{1,0:T(8,128)S(1)} %broadcast.74, f32[512,64]{1,0:T(8,128)} %get-tuple-element.20, f32[512,64]{1,0:T(8,128)S(1)} %broadcast.74, f32[512,64]{1,0:T(8,128)} %get-tuple-element.19, f32[512,64]{1,0:T(8,128)S(1)} %broadcast.74, f32[512,64]{1,0:T(8,128)} %get-tuple-element.18, ...), dimensions={1} | concatenate | bytes 2097152 | tf_op jit(solution)/shard_map/concatenate | solution.py:172
  40.3 68.7 %all-gather.4.cloned.1.call-done.kv_ref = bf16[8,513,512]{2,1,0:T(8,128)(2,1)} async-done(((bf16[1,513,512]{2,1,0:T(8,128)(2,1)}), bf16[8,513,512]{2,1,0:T(8,128)(2,1)}) %all-gather.4.cloned.1.call-update) | async-done | bytes 4202512 | tf_op jit(solution)/shard_map/all_gather | solution.py:194
  109.0 0.8 slice.100
  109.9 0.6 copy.22
  110.5 1.3 convert_reduce_fusion
  111.8 1.2 pad_add_fusion.bounds_ref
  113.0 15.9 %shard_map.113 = bf16[512,256]{1,0:T(8,128)(2,1)} custom-call(s32[3]{0:T(128)} %pad_add_fusion.bounds_ref, f32[512,512]{1,0:T(8,128)} %concatenate.16.proj_ref, bf16[8,513,512]{2,1,0:T(8,128)(2,1)} %all-gather.4.cloned.1.call-done.kv_ref, f32[4,1,128]{2,1,0:T(1,128)} %bitcast.84, s32[512,1]{1,0:T(8,128)} %copy.19.qseg_ref, s32[1,4096]{1,0:T(1,128)} %bitcast.81), custom_call_target="tpu_custom_call" | custom-call | flops 4294967296 | bytes 4194304 | tf_op jit(solution)/shard_map/pallas_call | solution.py:130
  128.9 1.7 convolution_convert_fusion.1
  130.6 0.0 copy-start.7
  130.6 1.1 copy-done.1
  131.7 1.0 dynamic-slice_bitcast_fusion.5
  132.7 1.5 collective-permute-start.4
  134.2 1.4 collective-permute-start.5
  135.6 6.8 %collective-permute-done.3 = bf16[128,1280]{1,0:T(8,128)(2,1)} collective-permute-done((bf16[128,1280]{1,0:T(8,128)(2,1)}, bf16[128,1280]{1,0:T(8,128)(2,1)}, u32[]{:S(2)}, u32[]{:S(2)}) %collective-permute-start.3) | collective-permute-done | bytes 327712 | tf_op jit(solution)/shard_map/ppermute | solution.py:43
  142.4 1.1 collective-permute-done.4
  143.5 5.5 %collective-permute-done.5 = bf16[128,1280]{1,0:T(8,128)(2,1)} collective-permute-done((bf16[128,1280]{1,0:T(8,128)(2,1)}, bf16[128,1280]{1,0:T(8,128)(2,1)}, u32[]{:S(2)}, u32[]{:S(2)}) %collective-permute-start.5) | collective-permute-done | bytes 327712 | tf_op jit(solution)/shard_map/ppermute | solution.py:43
  149.0 1.5 multiply_reduce_fusion.3
  150.5 1.8 multiply_reduce_fusion.2
  152.3 0.0 copy-start.12
  152.4 0.1 broadcast.73
  152.5 0.1 constant_dynamic-update-slice_fusion.3
  152.6 0.6 copy-done.2
  153.2 0.8 collective-permute-start.6
  154.0 0.2 select_reduce_fusion
  154.2 1.5 collective-permute-start.7
  155.8 0.2 collective-permute-start.8
  156.0 5.8 %collective-permute-done.6 = bf16[128,1280]{1,0:T(8,128)(2,1)S(1)} collective-permute-done((bf16[128,1280]{1,0:T(8,128)(2,1)S(1)}, bf16[128,1280]{1,0:T(8,128)(2,1)S(1)}, u32[]{:S(2)}, u32[]{:S(2)}) %collective-permute-start.6) | collective-permute-done | bytes 327712 | tf_op jit(solution)/shard_map/ppermute | solution.py:30
  161.8 3.1 %collective-permute-done.7 = bf16[128,1280]{1,0:T(8,128)(2,1)S(1)} collective-permute-done((bf16[128,1280]{1,0:T(8,128)(2,1)S(1)}, bf16[128,1280]{1,0:T(8,128)(2,1)S(1)}, u32[]{:S(2)}, u32[]{:S(2)}) %collective-permute-start.7) | collective-permute-done | bytes 327712 | tf_op jit(solution)/shard_map/ppermute | solution.py:30
  164.9 3.5 %collective-permute-done.8 = bf16[128,1280]{1,0:T(8,128)(2,1)S(1)} collective-permute-done((bf16[128,1280]{1,0:T(8,128)(2,1)S(1)}, bf16[128,1280]{1,0:T(8,128)(2,1)S(1)}, u32[]{:S(2)}, u32[]{:S(2)}) %collective-permute-start.8) | collective-permute-done | bytes 327712 | tf_op jit(solution)/shard_map/ppermute | solution.py:30
  168.5 6.4 %fusion = f32[512,2,1280]{2,0,1:T(8,128)S(1)} fusion(bf16[1280,2,1280]{2,1,0:T(2,128)(2,1)} %param.15, bf16[512,1280]{1,0:T(8,128)(2,1)S(1)} %constant_dynamic-update-slice_fusion), kind=kOutput, calls=%fused_computation | convolution fusion | flops 3355443200 | bytes 13107200 | tf_op jit(solution)/shard_map/td,dkf->tkf/dot_general | solution.py:246
  174.8 2.4 %convolution_convert_fusion = bf16[512,1280]{1,0:T(8,128)(2,1)S(1)} fusion(bf16[1280,1280]{1,0:T(8,128)(2,1)S(1)} %copy-done, f32[512,2,1280]{2,0,1:T(8,128)S(1)} %fusion, f32[1280]{0:T(1024)S(1)} %get-tuple-element.5, f32[1280]{0:T(1024)S(1)} %get-tuple-element.4), kind=kOutput, calls=%fused_computation.2 | convolution fusion | flops 1684275200 | bytes 9840640 | tf_op jit(solution)/shard_map/dot_general | solution.py:252
  177.3 1.1 copy-done.4
  178.4 1.0 dynamic-slice_bitcast_fusion.2
  179.3 1.5 collective-permute-start.10
  180.8 1.6 collective-permute-start.11
  182.5 0.7 fusion.21
  193.5 1.4 constant_dynamic-slice_fusion.3
  194.9 0.9 pad_maximum_fusion
  195.8 0.3 collective-permute-done.11
  196.1 1.1 collective-permute-done.9
  197.3 1.4 multiply_reduce_fusion.1
  198.7 1.6 multiply_reduce_fusion
  200.3 0.9 multiply_convert_fusion
  (39 shorter events, 0.3 us)
Async XLA Ops:
  7.2 167.7 %copy-start = (bf16[1280,1280]{1,0:T(8,128)(2,1)S(1)}, bf16[1280,1280]{1,0:T(8,128)(2,1)}, u32[]{:S(2)}) copy-start(bf16[1280,1280]{1,0:T(8,128)(2,1)} %param.16) | copy-start | bytes 9830404
  7.2 101.8 %all-gather.4.cloned.1.call-start = ((), (), s32[]{:S(2)}) async-start(), calls=%async_computation | async-start | bytes 4792320 | tf_op jit(solution)/shard_map/all_gather | solution.py:194
  7.2 6.4 %copy-start.9 = (s32[512]{0:T(512)S(1)}, s32[512]{0:T(512)}, u32[]{:S(2)}) copy-start(s32[512]{0:T(512)} %param.11) | copy-start | bytes 6148
  8.5 1.2 copy-start.6
  10.7 9.8 %collective-permute-start = (bf16[128,1280]{1,0:T(8,128)(2,1)}, bf16[128,1280]{1,0:T(8,128)(2,1)}, u32[]{:S(2)}, u32[]{:S(2)}) collective-permute-start(bf16[128,1280]{1,0:T(8,128)(2,1)} %get-tuple-element.13), channel_id=1, source_target_pairs={{0,1},{1,2},{2,3},{3,0},{4,5},{5,6},{6,7},{7,4},{8,9},{9,10},{10,1... | collective-permute-start | bytes 983048 | tf_op jit(solution)/shard_map/ppermute | solution.py:30
  10.7 11.5 %collective-permute-start.1 = (bf16[128,1280]{1,0:T(8,128)(2,1)}, bf16[128,1280]{1,0:T(8,128)(2,1)}, u32[]{:S(2)}, u32[]{:S(2)}) collective-permute-start(bf16[128,1280]{1,0:T(8,128)(2,1)} %get-tuple-element.13), channel_id=1, source_target_pairs={{0,2},{1,3},{2,0},{3,1},{4,6},{5,7},{6,4},{7,5},{8,10},{9,11},{10,... | collective-permute-start | bytes 983048 | tf_op jit(solution)/shard_map/ppermute | solution.py:30
  12.2 14.8 %collective-permute-start.2 = (bf16[128,1280]{1,0:T(8,128)(2,1)}, bf16[128,1280]{1,0:T(8,128)(2,1)}, u32[]{:S(2)}, u32[]{:S(2)}) collective-permute-start(bf16[128,1280]{1,0:T(8,128)(2,1)} %get-tuple-element.13), channel_id=1, source_target_pairs={{0,3},{1,0},{2,1},{3,2},{4,7},{5,4},{6,5},{7,6},{8,11},{9,8},{10,9... | collective-permute-start | bytes 983048 | tf_op jit(solution)/shard_map/ppermute | solution.py:30
  13.7 15.1 %copy-start.11 = (bf16[1280,4,192]{0,2,1:T(8,128)(2,1)S(1)}, bf16[1280,4,192]{0,2,1:T(8,128)(2,1)}, u32[]{:S(2)}) copy-start(bf16[1280,4,192]{0,2,1:T(8,128)(2,1)} %param.13) | copy-start | bytes 5898244
  32.5 2.5 %copy-start.10 = (f32[4,64]{1,0:T(4,128)S(1)}, f32[4,64]{1,0:T(4,128)}, u32[]{:S(2)}) copy-start(f32[4,64]{1,0:T(4,128)} %param.17) | copy-start | bytes 3076
  130.6 1.1 copy-start.1
  130.6 5.0 %copy-start.7 = (f32[2,1280]{1,0:T(2,128)S(1)}, f32[2,1280]{1,0:T(2,128)}, u32[]{:S(2)}) copy-start(f32[2,1280]{1,0:T(2,128)} %param.19) | copy-start | bytes 30724
  132.7 9.8 %collective-permute-start.3 = (bf16[128,1280]{1,0:T(8,128)(2,1)}, bf16[128,1280]{1,0:T(8,128)(2,1)}, u32[]{:S(2)}, u32[]{:S(2)}) collective-permute-start(bf16[128,1280]{1,0:T(8,128)(2,1)} %get-tuple-element.25), channel_id=1, source_target_pairs={{0,1},{1,2},{2,3},{3,0},{4,5},{5,6},{6,7},{7,4},{8,9},{9,10},{10,1... | collective-permute-start | bytes 983048 | tf_op jit(solution)/shard_map/ppermute | solution.py:43
  132.7 10.9 %collective-permute-start.4 = (bf16[128,1280]{1,0:T(8,128)(2,1)}, bf16[128,1280]{1,0:T(8,128)(2,1)}, u32[]{:S(2)}, u32[]{:S(2)}) collective-permute-start(bf16[128,1280]{1,0:T(8,128)(2,1)} %get-tuple-element.27), channel_id=1, source_target_pairs={{0,2},{1,3},{2,0},{3,1},{4,6},{5,7},{6,4},{7,5},{8,10},{9,11},{10,... | collective-permute-start | bytes 983048 | tf_op jit(solution)/shard_map/ppermute | solution.py:43
  134.2 14.8 %collective-permute-start.5 = (bf16[128,1280]{1,0:T(8,128)(2,1)}, bf16[128,1280]{1,0:T(8,128)(2,1)}, u32[]{:S(2)}, u32[]{:S(2)}) collective-permute-start(bf16[128,1280]{1,0:T(8,128)(2,1)} %get-tuple-element.26), channel_id=1, source_target_pairs={{0,3},{1,0},{2,1},{3,2},{4,7},{5,4},{6,5},{7,6},{8,11},{9,8},{10,9... | collective-permute-start | bytes 983048 | tf_op jit(solution)/shard_map/ppermute | solution.py:43
  152.3 0.8 copy-start.2
  152.3 1.7 copy-start.12
  152.4 3.4 %copy-start.8 = (f32[2,1280]{1,0:T(2,128)S(1)}, f32[2,1280]{1,0:T(2,128)}, u32[]{:S(2)}) copy-start(f32[2,1280]{1,0:T(2,128)} %param.18) | copy-start | bytes 30724
  153.2 8.6 %collective-permute-start.6 = (bf16[128,1280]{1,0:T(8,128)(2,1)S(1)}, bf16[128,1280]{1,0:T(8,128)(2,1)S(1)}, u32[]{:S(2)}, u32[]{:S(2)}) collective-permute-start(bf16[128,1280]{1,0:T(8,128)(2,1)S(1)} %get-tuple-element.9), channel_id=1, source_target_pairs={{0,1},{1,2},{2,3},{3,0},{4,5},{5,6},{6,7},{7,4},{8,9},{9,10},{10,1... | collective-permute-start | bytes 983048 | tf_op jit(solution)/shard_map/ppermute | solution.py:30
  154.2 10.7 %collective-permute-start.7 = (bf16[128,1280]{1,0:T(8,128)(2,1)S(1)}, bf16[128,1280]{1,0:T(8,128)(2,1)S(1)}, u32[]{:S(2)}, u32[]{:S(2)}) collective-permute-start(bf16[128,1280]{1,0:T(8,128)(2,1)S(1)} %get-tuple-element.9), channel_id=1, source_target_pairs={{0,2},{1,3},{2,0},{3,1},{4,6},{5,7},{6,4},{7,5},{8,10},{9,11},{10,... | collective-permute-start | bytes 983048 | tf_op jit(solution)/shard_map/ppermute | solution.py:30
  155.8 12.7 %collective-permute-start.8 = (bf16[128,1280]{1,0:T(8,128)(2,1)S(1)}, bf16[128,1280]{1,0:T(8,128)(2,1)S(1)}, u32[]{:S(2)}, u32[]{:S(2)}) collective-permute-start(bf16[128,1280]{1,0:T(8,128)(2,1)S(1)} %get-tuple-element.9), channel_id=1, source_target_pairs={{0,3},{1,0},{2,1},{3,2},{4,7},{5,4},{6,5},{7,6},{8,11},{9,8},{10,9... | collective-permute-start | bytes 983048 | tf_op jit(solution)/shard_map/ppermute | solution.py:30
  177.3 1.1 copy-start.4
  179.3 16.4 %collective-permute-start.10 = (bf16[128,1280]{1,0:T(8,128)(2,1)}, bf16[128,1280]{1,0:T(8,128)(2,1)}, u32[]{:S(2)}, u32[]{:S(2)}) collective-permute-start(bf16[128,1280]{1,0:T(8,128)(2,1)} %get-tuple-element.24), channel_id=1, source_target_pairs={{0,2},{1,3},{2,0},{3,1},{4,6},{5,7},{6,4},{7,5},{8,10},{9,11},{10,... | collective-permute-start | bytes 983048 | tf_op jit(solution)/shard_map/ppermute | solution.py:43
  180.8 15.3 %collective-permute-start.11 = (bf16[128,1280]{1,0:T(8,128)(2,1)}, bf16[128,1280]{1,0:T(8,128)(2,1)}, u32[]{:S(2)}, u32[]{:S(2)}) collective-permute-start(bf16[128,1280]{1,0:T(8,128)(2,1)} %get-tuple-element.23), channel_id=1, source_target_pairs={{0,3},{1,0},{2,1},{3,2},{4,7},{5,4},{6,5},{7,6},{8,11},{9,8},{10,9... | collective-permute-start | bytes 983048 | tf_op jit(solution)/shard_map/ppermute | solution.py:43
  182.5 14.8 %collective-permute-start.9 = (bf16[128,1280]{1,0:T(8,128)(2,1)}, bf16[128,1280]{1,0:T(8,128)(2,1)}, u32[]{:S(2)}, u32[]{:S(2)}) collective-permute-start(bf16[128,1280]{1,0:T(8,128)(2,1)} %get-tuple-element.22), channel_id=1, source_target_pairs={{0,1},{1,2},{2,3},{3,0},{4,5},{5,6},{6,7},{7,4},{8,9},{9,10},{10,1... | collective-permute-start | bytes 983048 | tf_op jit(solution)/shard_map/ppermute | solution.py:43
  193.5 3.7 %copy-start.5 = (bf16[512,1280]{1,0:T(8,128)(2,1)S(1)}, bf16[512,1280]{1,0:T(8,128)(2,1)}, u32[]{:S(2)}) copy-start(bf16[512,1280]{1,0:T(8,128)(2,1)} %copy-done.4) | copy-start | bytes 3932164
  194.9 3.8 %copy-start.3 = (f32[128,1280]{1,0:T(8,128)S(1)}, f32[128,1280]{1,0:T(8,128)}, u32[]{:S(2)}) copy-start(f32[128,1280]{1,0:T(8,128)} %copy-done.2) | copy-start | bytes 1966084
Sparse Core Ops, SparseCore 0:
  33.6 75.2 all-gather.3

commit v2 on v1

--- a/solution.py
+++ b/solution.py
@@ -87,14 +87,13 @@
                 k_unit = (
                     kv_f * lax.rsqrt(jnp.sum(k_sq, axis=1, keepdims=True) + EPSILON) * scale
                 ).astype(jnp.bfloat16)
-                k_seg = kseg_ref[:, pl.ds(key_at, K_TILE)]
                 scores = lax.dot_general(
                     q_tile, k_unit, (((1,), (1,)), ((), ())), preferred_element_type=jnp.float32
                 )
                 if not fold:
                     scores = factor * scores
                 k_pos = key_at + lax.broadcasted_iota(jnp.int32, (Q_TILE, K_TILE), 1)
-                allowed = (q_seg == k_seg) & (k_pos <= q_pos)
+                allowed = (k_pos >= q_seg) & (k_pos <= q_pos)
                 weights = jnp.where(allowed, jnp.exp(scores - shift), 0.0).astype(jnp.bfloat16)
                 kv_sum = jnp.where(key_lane == 0, jnp.ones_like(kv_blk), kv_blk)
                 return acc + jnp.dot(weights, kv_sum, preferred_element_type=jnp.float32)
@@ -208,12 +207,15 @@
     )
     block_hi = (tile_first + Q_TILE - 1) // K_TILE
     bounds = jnp.concatenate([block_lo, block_hi, first_token[None]]).astype(jnp.int32)
+    segment_start = jnp.sum(
+        (seg_piece[None, :] < segment_ids[:, None]).astype(jnp.int32), axis=1
+    )
     heads_pad = flash_attend(
         bounds,
         query_pad,
         gathered,
         scale_pad,
-        segment_ids.reshape(local_tokens, 1),
+        segment_start.reshape(local_tokens, 1),
         seg_piece.reshape(1, piece_rows),
         math.sqrt(head_dim),
         head_dim,

time: 210 us -> 212 us (level)
  the two profiles are of different devices: /device:TPU:10 before, /device:TPU:26 now
where the time goes in v2:
time: 212 us; the launch traced here: 209 us
  waiting for transfers between devices  106 us (50%)
  between operations  24.5 us (12%)
  local copies, waits for them, and re-layouts  21.5 us (10%)
  Pallas kernels  15.9 us (8%)
  other arithmetic  15.1 us (7%)
  matrix products  14.2 us (7%)
  starting transfers between devices  11.6 us (5%)
    all_gather x1, waiting for transfers between devices, body(): gathered = lax.all_gather(kv_ext, 'seq', axis=0, tiled=False)  68.4 us
    ppermute x6, waiting for transfers between devices, gather_rows(): came = lax.ppermute(part, axis, pairs)  22.3 us
    pallas_call x1, Pallas kernels, flash_attend(): pl.pallas_call(functools.partial(attend_kernel, factor=factor, half=half)...  15.9 us
    ppermute x6, waiting for transfers between devices, scatter_sum(): total = total + lax.ppermute(send, axis, pairs).astype(jnp.float32)  15.2 us
    reduce_sum x5, other arithmetic, unit_rows(): jnp.sum(matrix * matrix, axis=-1, keepdims=True) + EPSILON  7.59 us
    dot_general x1, matrix products, body(): jnp.einsum('td,dkf->tkf', mid_rows, up_proj, preferred_element_type=jnp.f...  6.37 us
    ppermute x6, starting transfers between devices, scatter_sum(): total = total + lax.ppermute(send, axis, pairs).astype(jnp.float32)  5.98 us
    ppermute x6, starting transfers between devices, gather_rows(): came = lax.ppermute(part, axis, pairs)  5.56 us
  transfers between devices with their start and end apart: 13, of which 11 were waited for; matrix products, arithmetic and copies ran while one was open for 6% of the time, Pallas kernels for 0%

profile of v2, /device:TPU:26, one launch (start us, length us, event | category | flops | bytes accessed | tf_op | source)
XLA Modules:
  0.0 208.8 jit_solution(2927504722627178329)
XLA Ops:
  7.2 0.0 copy-start
  7.2 0.0 all-gather.4.cloned.1.call-start
  7.2 1.3 fusion.9
  8.5 1.2 broadcast.74.clone
  9.7 1.0 constant_dynamic-update-slice_fusion.7
  10.7 1.5 collective-permute-start.1
  12.2 1.4 collective-permute-start.2
  13.7 0.0 copy-start.11
  13.7 6.8 %collective-permute-done = bf16[128,1280]{1,0:T(8,128)(2,1)} collective-permute-done((bf16[128,1280]{1,0:T(8,128)(2,1)}, bf16[128,1280]{1,0:T(8,128)(2,1)}, u32[]{:S(2)}, u32[]{:S(2)}) %collective-permute-start) | collective-permute-done | bytes 327712 | tf_op jit(solution)/shard_map/ppermute | solution.py:30
  20.4 1.7 constant_dynamic-update-slice_fusion.6
  22.2 1.7 constant_dynamic-update-slice_fusion.5
  23.9 3.2 %collective-permute-done.2 = bf16[128,1280]{1,0:T(8,128)(2,1)} collective-permute-done((bf16[128,1280]{1,0:T(8,128)(2,1)}, bf16[128,1280]{1,0:T(8,128)(2,1)}, u32[]{:S(2)}, u32[]{:S(2)}) %collective-permute-start.2) | collective-permute-done | bytes 327712 | tf_op jit(solution)/shard_map/ppermute | solution.py:30
  27.0 1.7 constant_dynamic-update-slice_fusion.4
  28.8 3.7 %fusion.22 = (bf16[512,768]{1,0:T(8,128)(2,1)S(1)}, f32[512,768]{1,0:T(8,128)}) fusion(bf16[512,1280]{1,0:T(8,128)(2,1)} %constant_dynamic-update-slice_fusion.4, bf16[1280,768]{0,1:T(8,128)(2,1)S(1)} %bitcast.90), kind=kOutput, calls=%fused_computation.75 | convolution fusion | flops 1007026176 | bytes 5636096 | tf_op jit(solution)/shard_map/dot_general | solution.py:165
  32.5 0.1 fusion.20
  32.6 0.9 maximum_bitcast_fusion
  33.5 0.0 all-gather.4.cloned.1.call-update
  33.6 0.5 slice.102
  34.1 0.6 pad.4
  34.7 2.3 %fusion.19 = (f32[512,64]{1,0:T(8,128)}, f32[512,64]{1,0:T(8,128)}, f32[512,64]{1,0:T(8,128)}, f32[512,64]{1,0:T(8,128)}) fusion(f32[512,768]{1,0:T(8,128)} %get-tuple-element.40), kind=kLoop, calls=%fused_computation.72 | loop fusion | bytes 1048576 | tf_op jit(solution)/shard_map/slice | solution.py:175
  37.0 2.3 %concatenate.16.proj_ref = f32[512,512]{1,0:T(8,128)} concatenate(f32[512,64]{1,0:T(8,128)} %get-tuple-element.21, f32[512,64]{1,0:T(8,128)S(1)} %broadcast.75, f32[512,64]{1,0:T(8,128)} %get-tuple-element.20, f32[512,64]{1,0:T(8,128)S(1)} %broadcast.75, f32[512,64]{1,0:T(8,128)} %get-tuple-element.19, f32[512,64]{1,0:T(8,128)S(1)} %broadcast.75, f32[512,64]{1,0:T(8,128)} %get-tuple-element.18, ...), dimensions={1} | concatenate | bytes 2097152 | tf_op jit(solution)/shard_map/concatenate | solution.py:171
  39.3 68.4 %all-gather.4.cloned.1.call-done.kv_ref = bf16[8,513,512]{2,1,0:T(8,128)(2,1)} async-done(((bf16[1,513,512]{2,1,0:T(8,128)(2,1)}), bf16[8,513,512]{2,1,0:T(8,128)(2,1)}) %all-gather.4.cloned.1.call-update) | async-done | bytes 4202512 | tf_op jit(solution)/shard_map/all_gather | solution.py:193
  107.8 0.8 slice.100
  108.6 1.0 convert_reduce_fusion
  109.7 0.9 copy.19.qseg_ref
  110.5 0.6 copy.23
  111.1 1.4 convert_reduce_fusion.1
  112.5 1.3 pad_add_fusion.bounds_ref
  113.8 15.9 %shard_map.113 = bf16[512,256]{1,0:T(8,128)(2,1)} custom-call(s32[3]{0:T(128)} %pad_add_fusion.bounds_ref, f32[512,512]{1,0:T(8,128)} %concatenate.16.proj_ref, bf16[8,513,512]{2,1,0:T(8,128)(2,1)} %all-gather.4.cloned.1.call-done.kv_ref, f32[4,1,128]{2,1,0:T(1,128)} %bitcast.89, s32[512,1]{1,0:T(8,128)} %copy.19.qseg_ref, s32[1,4096]{1,0:T(1,128)} %bitcast.85), custom_call_target="tpu_custom_call" | custom-call | flops 4294967296 | bytes 4194304 | tf_op jit(solution)/shard_map/pallas_call | solution.py:129
  129.7 1.7 convolution_convert_fusion.1
  131.4 0.0 copy-start.7
  131.4 1.1 copy-done.1
  132.5 1.0 dynamic-slice_bitcast_fusion.5
  133.4 1.5 collective-permute-start.4
  134.9 1.4 collective-permute-start.5
  136.4 6.8 %collective-permute-done.3 = bf16[128,1280]{1,0:T(8,128)(2,1)} collective-permute-done((bf16[128,1280]{1,0:T(8,128)(2,1)}, bf16[128,1280]{1,0:T(8,128)(2,1)}, u32[]{:S(2)}, u32[]{:S(2)}) %collective-permute-start.3) | collective-permute-done | bytes 327712 | tf_op jit(solution)/shard_map/ppermute | solution.py:43
  143.2 1.1 collective-permute-done.4
  144.3 5.4 %collective-permute-done.5 = bf16[128,1280]{1,0:T(8,128)(2,1)} collective-permute-done((bf16[128,1280]{1,0:T(8,128)(2,1)}, bf16[128,1280]{1,0:T(8,128)(2,1)}, u32[]{:S(2)}, u32[]{:S(2)}) %collective-permute-start.5) | collective-permute-done | bytes 327712 | tf_op jit(solution)/shard_map/ppermute | solution.py:43
  149.8 1.5 multiply_reduce_fusion.3
  151.3 1.8 multiply_reduce_fusion.2
  153.1 0.1 broadcast.74
  153.2 0.1 constant_dynamic-update-slice_fusion.3
  153.3 0.6 copy-done.2
  153.9 0.9 collective-permute-start.6
  154.8 0.2 select_reduce_fusion
  155.0 1.5 collective-permute-start.7
  156.5 0.2 collective-permute-start.8
  156.8 5.8 %collective-permute-done.6 = bf16[128,1280]{1,0:T(8,128)(2,1)S(1)} collective-permute-done((bf16[128,1280]{1,0:T(8,128)(2,1)S(1)}, bf16[128,1280]{1,0:T(8,128)(2,1)S(1)}, u32[]{:S(2)}, u32[]{:S(2)}) %collective-permute-start.6) | collective-permute-done | bytes 327712 | tf_op jit(solution)/shard_map/ppermute | solution.py:30
  162.6 3.1 %collective-permute-done.7 = bf16[128,1280]{1,0:T(8,128)(2,1)S(1)} collective-permute-done((bf16[128,1280]{1,0:T(8,128)(2,1)S(1)}, bf16[128,1280]{1,0:T(8,128)(2,1)S(1)}, u32[]{:S(2)}, u32[]{:S(2)}) %collective-permute-start.7) | collective-permute-done | bytes 327712 | tf_op jit(solution)/shard_map/ppermute | solution.py:30
  165.7 3.5 %collective-permute-done.8 = bf16[128,1280]{1,0:T(8,128)(2,1)S(1)} collective-permute-done((bf16[128,1280]{1,0:T(8,128)(2,1)S(1)}, bf16[128,1280]{1,0:T(8,128)(2,1)S(1)}, u32[]{:S(2)}, u32[]{:S(2)}) %collective-permute-start.8) | collective-permute-done | bytes 327712 | tf_op jit(solution)/shard_map/ppermute | solution.py:30
  169.3 6.4 %fusion = f32[512,2,1280]{2,0,1:T(8,128)S(1)} fusion(bf16[1280,2,1280]{2,1,0:T(2,128)(2,1)} %param.15, bf16[512,1280]{1,0:T(8,128)(2,1)S(1)} %constant_dynamic-update-slice_fusion), kind=kOutput, calls=%fused_computation.1 | convolution fusion | flops 3355443200 | bytes 13107200 | tf_op jit(solution)/shard_map/td,dkf->tkf/dot_general | solution.py:248
  175.6 2.4 %convolution_convert_fusion = bf16[512,1280]{1,0:T(8,128)(2,1)S(1)} fusion(bf16[1280,1280]{1,0:T(8,128)(2,1)S(1)} %copy-done, f32[512,2,1280]{2,0,1:T(8,128)S(1)} %fusion, f32[1280]{0:T(1024)S(1)} %get-tuple-element.5, f32[1280]{0:T(1024)S(1)} %get-tuple-element.4), kind=kOutput, calls=%fused_computation.3 | convolution fusion | flops 1684275200 | bytes 9840640 | tf_op jit(solution)/shard_map/dot_general | solution.py:254
  178.1 1.1 copy-done.4
  179.2 1.0 dynamic-slice_bitcast_fusion.2
  180.1 1.5 collective-permute-start.10
  181.6 1.6 collective-permute-start.11
  183.2 0.7 fusion.21
  194.0 1.4 constant_dynamic-slice_fusion.3
  195.4 0.9 pad_maximum_fusion
  196.2 0.7 collective-permute-done.11
  196.9 1.2 collective-permute-done.9
  198.1 1.4 multiply_reduce_fusion.1
  199.5 1.6 multiply_reduce_fusion
  201.1 0.9 multiply_convert_fusion
  (41 shorter events, 0.3 us)
Async XLA Ops:
  7.2 168.5 %copy-start = (bf16[1280,1280]{1,0:T(8,128)(2,1)S(1)}, bf16[1280,1280]{1,0:T(8,128)(2,1)}, u32[]{:S(2)}) copy-start(bf16[1280,1280]{1,0:T(8,128)(2,1)} %param.16) | copy-start | bytes 9830404
  7.2 100.6 %all-gather.4.cloned.1.call-start = ((), (), s32[]{:S(2)}) async-start(), calls=%async_computation | async-start | bytes 4792320 | tf_op jit(solution)/shard_map/all_gather | solution.py:193
  7.2 6.4 %copy-start.9 = (s32[512]{0:T(512)S(1)}, s32[512]{0:T(512)}, u32[]{:S(2)}) copy-start(s32[512]{0:T(512)} %param.11) | copy-start | bytes 6148
  8.5 1.2 copy-start.6
  10.7 9.8 %collective-permute-start = (bf16[128,1280]{1,0:T(8,128)(2,1)}, bf16[128,1280]{1,0:T(8,128)(2,1)}, u32[]{:S(2)}, u32[]{:S(2)}) collective-permute-start(bf16[128,1280]{1,0:T(8,128)(2,1)} %get-tuple-element.13), channel_id=1, source_target_pairs={{0,1},{1,2},{2,3},{3,0},{4,5},{5,6},{6,7},{7,4},{8,9},{9,10},{10,1... | collective-permute-start | bytes 983048 | tf_op jit(solution)/shard_map/ppermute | solution.py:30
  10.7 11.5 %collective-permute-start.1 = (bf16[128,1280]{1,0:T(8,128)(2,1)}, bf16[128,1280]{1,0:T(8,128)(2,1)}, u32[]{:S(2)}, u32[]{:S(2)}) collective-permute-start(bf16[128,1280]{1,0:T(8,128)(2,1)} %get-tuple-element.13), channel_id=1, source_target_pairs={{0,2},{1,3},{2,0},{3,1},{4,6},{5,7},{6,4},{7,5},{8,10},{9,11},{10,... | collective-permute-start | bytes 983048 | tf_op jit(solution)/shard_map/ppermute | solution.py:30
  12.2 14.8 %collective-permute-start.2 = (bf16[128,1280]{1,0:T(8,128)(2,1)}, bf16[128,1280]{1,0:T(8,128)(2,1)}, u32[]{:S(2)}, u32[]{:S(2)}) collective-permute-start(bf16[128,1280]{1,0:T(8,128)(2,1)} %get-tuple-element.13), channel_id=1, source_target_pairs={{0,3},{1,0},{2,1},{3,2},{4,7},{5,4},{6,5},{7,6},{8,11},{9,8},{10,9... | collective-permute-start | bytes 983048 | tf_op jit(solution)/shard_map/ppermute | solution.py:30
  13.7 15.1 %copy-start.11 = (bf16[1280,4,192]{0,2,1:T(8,128)(2,1)S(1)}, bf16[1280,4,192]{0,2,1:T(8,128)(2,1)}, u32[]{:S(2)}) copy-start(bf16[1280,4,192]{0,2,1:T(8,128)(2,1)} %param.13) | copy-start | bytes 5898244
  32.5 1.6 copy-start.10
  131.4 1.1 copy-start.1
  131.4 5.0 %copy-start.7 = (f32[2,1280]{1,0:T(2,128)S(1)}, f32[2,1280]{1,0:T(2,128)}, u32[]{:S(2)}) copy-start(f32[2,1280]{1,0:T(2,128)} %param.19) | copy-start | bytes 30724
  133.4 9.8 %collective-permute-start.3 = (bf16[128,1280]{1,0:T(8,128)(2,1)}, bf16[128,1280]{1,0:T(8,128)(2,1)}, u32[]{:S(2)}, u32[]{:S(2)}) collective-permute-start(bf16[128,1280]{1,0:T(8,128)(2,1)} %get-tuple-element.25), channel_id=1, source_target_pairs={{0,1},{1,2},{2,3},{3,0},{4,5},{5,6},{6,7},{7,4},{8,9},{9,10},{10,1... | collective-permute-start | bytes 983048 | tf_op jit(solution)/shard_map/ppermute | solution.py:43
  133.4 10.9 %collective-permute-start.4 = (bf16[128,1280]{1,0:T(8,128)(2,1)}, bf16[128,1280]{1,0:T(8,128)(2,1)}, u32[]{:S(2)}, u32[]{:S(2)}) collective-permute-start(bf16[128,1280]{1,0:T(8,128)(2,1)} %get-tuple-element.27), channel_id=1, source_target_pairs={{0,2},{1,3},{2,0},{3,1},{4,6},{5,7},{6,4},{7,5},{8,10},{9,11},{10,... | collective-permute-start | bytes 983048 | tf_op jit(solution)/shard_map/ppermute | solution.py:43
  134.9 14.8 %collective-permute-start.5 = (bf16[128,1280]{1,0:T(8,128)(2,1)}, bf16[128,1280]{1,0:T(8,128)(2,1)}, u32[]{:S(2)}, u32[]{:S(2)}) collective-permute-start(bf16[128,1280]{1,0:T(8,128)(2,1)} %get-tuple-element.26), channel_id=1, source_target_pairs={{0,3},{1,0},{2,1},{3,2},{4,7},{5,4},{6,5},{7,6},{8,11},{9,8},{10,9... | collective-permute-start | bytes 983048 | tf_op jit(solution)/shard_map/ppermute | solution.py:43
  153.1 0.8 copy-start.2
  153.1 1.7 copy-start.12
  153.1 3.4 %copy-start.8 = (f32[2,1280]{1,0:T(2,128)S(1)}, f32[2,1280]{1,0:T(2,128)}, u32[]{:S(2)}) copy-start(f32[2,1280]{1,0:T(2,128)} %param.18) | copy-start | bytes 30724
  153.9 8.6 %collective-permute-start.6 = (bf16[128,1280]{1,0:T(8,128)(2,1)S(1)}, bf16[128,1280]{1,0:T(8,128)(2,1)S(1)}, u32[]{:S(2)}, u32[]{:S(2)}) collective-permute-start(bf16[128,1280]{1,0:T(8,128)(2,1)S(1)} %get-tuple-element.9), channel_id=1, source_target_pairs={{0,1},{1,2},{2,3},{3,0},{4,5},{5,6},{6,7},{7,4},{8,9},{9,10},{10,1... | collective-permute-start | bytes 983048 | tf_op jit(solution)/shard_map/ppermute | solution.py:30
  155.0 10.7 %collective-permute-start.7 = (bf16[128,1280]{1,0:T(8,128)(2,1)S(1)}, bf16[128,1280]{1,0:T(8,128)(2,1)S(1)}, u32[]{:S(2)}, u32[]{:S(2)}) collective-permute-start(bf16[128,1280]{1,0:T(8,128)(2,1)S(1)} %get-tuple-element.9), channel_id=1, source_target_pairs={{0,2},{1,3},{2,0},{3,1},{4,6},{5,7},{6,4},{7,5},{8,10},{9,11},{10,... | collective-permute-start | bytes 983048 | tf_op jit(solution)/shard_map/ppermute | solution.py:30
  156.5 12.7 %collective-permute-start.8 = (bf16[128,1280]{1,0:T(8,128)(2,1)S(1)}, bf16[128,1280]{1,0:T(8,128)(2,1)S(1)}, u32[]{:S(2)}, u32[]{:S(2)}) collective-permute-start(bf16[128,1280]{1,0:T(8,128)(2,1)S(1)} %get-tuple-element.9), channel_id=1, source_target_pairs={{0,3},{1,0},{2,1},{3,2},{4,7},{5,4},{6,5},{7,6},{8,11},{9,8},{10,9... | collective-permute-start | bytes 983048 | tf_op jit(solution)/shard_map/ppermute | solution.py:30
  178.1 1.1 copy-start.4
  180.1 16.1 %collective-permute-start.10 = (bf16[128,1280]{1,0:T(8,128)(2,1)}, bf16[128,1280]{1,0:T(8,128)(2,1)}, u32[]{:S(2)}, u32[]{:S(2)}) collective-permute-start(bf16[128,1280]{1,0:T(8,128)(2,1)} %get-tuple-element.24), channel_id=1, source_target_pairs={{0,2},{1,3},{2,0},{3,1},{4,6},{5,7},{6,4},{7,5},{8,10},{9,11},{10,... | collective-permute-start | bytes 983048 | tf_op jit(solution)/shard_map/ppermute | solution.py:43
  181.6 15.3 %collective-permute-start.11 = (bf16[128,1280]{1,0:T(8,128)(2,1)}, bf16[128,1280]{1,0:T(8,128)(2,1)}, u32[]{:S(2)}, u32[]{:S(2)}) collective-permute-start(bf16[128,1280]{1,0:T(8,128)(2,1)} %get-tuple-element.23), channel_id=1, source_target_pairs={{0,3},{1,0},{2,1},{3,2},{4,7},{5,4},{6,5},{7,6},{8,11},{9,8},{10,9... | collective-permute-start | bytes 983048 | tf_op jit(solution)/shard_map/ppermute | solution.py:43
  183.2 14.9 %collective-permute-start.9 = (bf16[128,1280]{1,0:T(8,128)(2,1)}, bf16[128,1280]{1,0:T(8,128)(2,1)}, u32[]{:S(2)}, u32[]{:S(2)}) collective-permute-start(bf16[128,1280]{1,0:T(8,128)(2,1)} %get-tuple-element.22), channel_id=1, source_target_pairs={{0,1},{1,2},{2,3},{3,0},{4,5},{5,6},{6,7},{7,4},{8,9},{9,10},{10,1... | collective-permute-start | bytes 983048 | tf_op jit(solution)/shard_map/ppermute | solution.py:43
  194.0 4.1 %copy-start.5 = (bf16[512,1280]{1,0:T(8,128)(2,1)S(1)}, bf16[512,1280]{1,0:T(8,128)(2,1)}, u32[]{:S(2)}) copy-start(bf16[512,1280]{1,0:T(8,128)(2,1)} %copy-done.4) | copy-start | bytes 3932164
  195.4 4.2 %copy-start.3 = (f32[128,1280]{1,0:T(8,128)S(1)}, f32[128,1280]{1,0:T(8,128)}, u32[]{:S(2)}) copy-start(f32[128,1280]{1,0:T(8,128)} %copy-done.2) | copy-start | bytes 1966084
Sparse Core Ops, SparseCore 0:
  33.6 74.0 all-gather.3

commit v3 on v1

--- a/solution.py
+++ b/solution.py
@@ -22,14 +22,12 @@
 def gather_rows(part, axis):
     count = lax.axis_size(axis)
     index = lax.axis_index(axis)
-    rows = part.shape[0]
-    out = jnp.zeros((count * rows, *part.shape[1:]), part.dtype)
-    out = lax.dynamic_update_slice_in_dim(out, part, index * rows, 0)
+    parts = [part]
     for shift in range(1, count):
         pairs = [(j, (j + shift) % count) for j in range(count)]
-        came = lax.ppermute(part, axis, pairs)
-        out = lax.dynamic_update_slice_in_dim(out, came, ((index - shift) % count) * rows, 0)
-    return out
+        parts.append(lax.ppermute(part, axis, pairs))
+    order = (index - jnp.arange(count, dtype=jnp.int32)) % count
+    return jnp.take(jnp.stack(parts), order, axis=0).reshape(-1, *part.shape[1:])
 
 
 def scatter_sum(whole, axis):

time: 210 us -> 211 us (level)
  the two profiles are of different devices: /device:TPU:10 before, /device:TPU:26 now
where the time goes in v3:
time: 211 us; the launch traced here: 210 us
  waiting for transfers between devices  105 us (50%)
  between operations  24.8 us (12%)
  other arithmetic  21.1 us (10%)
  local copies, waits for them, and re-layouts  19.1 us (9%)
  Pallas kernels  15.9 us (8%)
  matrix products  12.9 us (6%)
  starting transfers between devices  11.4 us (5%)
    all_gather x1, waiting for transfers between devices, body(): gathered = lax.all_gather(kv_ext, 'seq', axis=0, tiled=False)  66.2 us
    ppermute x6, waiting for transfers between devices, gather_rows(): parts.append(lax.ppermute(part, axis, pairs))  24.4 us
    pallas_call x1, Pallas kernels, flash_attend(): pl.pallas_call(functools.partial(attend_kernel, factor=factor, half=half)...  15.9 us
    ppermute x6, waiting for transfers between devices, scatter_sum(): total = total + lax.ppermute(send, axis, pairs).astype(jnp.float32)  14.3 us
    dot_general x1, matrix products, body(): jnp.einsum('td,dkf->tkf', mid_rows, up_proj, preferred_element_type=jnp.f...  6.35 us
    gather x2, local copies, waits for them, and re-layouts, gather_rows(): jnp.take(jnp.stack(parts), order, axis=0).reshape(-1, *part.shape[1:])  6.16 us
    ppermute x6, starting transfers between devices, scatter_sum(): total = total + lax.ppermute(send, axis, pairs).astype(jnp.float32)  6.05 us
    ppermute x6, starting transfers between devices, gather_rows(): parts.append(lax.ppermute(part, axis, pairs))  5.36 us
  transfers between devices with their start and end apart: 13, of which 12 were waited for; matrix products, arithmetic and copies ran while one was open for 6% of the time, Pallas kernels for 0%

profile of v3, /device:TPU:26, one launch (start us, length us, event | category | flops | bytes accessed | tf_op | source)
XLA Modules:
  0.0 210.2 jit_solution(4501405714949107241)
XLA Ops:
  7.2 0.0 all-gather.4.cloned.1.call-start
  7.2 1.3 fusion.8
  8.5 1.8 fusion.9
  10.3 1.6 collective-permute-start.1
  11.9 1.4 collective-permute-start.2
  13.4 0.7 convert_element_type.92
  14.1 1.1 fusion.29
  15.2 4.9 %collective-permute-done = bf16[128,1280]{1,0:T(8,128)(2,1)} collective-permute-done((bf16[128,1280]{1,0:T(8,128)(2,1)}, bf16[128,1280]{1,0:T(8,128)(2,1)}, u32[]{:S(2)}, u32[]{:S(2)}) %collective-permute-start) | collective-permute-done | bytes 327712 | tf_op jit(solution)/shard_map/ppermute | solution.py:28
  20.1 1.1 collective-permute-done.1
  21.2 5.5 %collective-permute-done.2 = bf16[128,1280]{1,0:T(8,128)(2,1)} collective-permute-done((bf16[128,1280]{1,0:T(8,128)(2,1)}, bf16[128,1280]{1,0:T(8,128)(2,1)}, u32[]{:S(2)}, u32[]{:S(2)}) %collective-permute-start.2) | collective-permute-done | bytes 327712 | tf_op jit(solution)/shard_map/ppermute | solution.py:28
  26.7 2.4 %pad_maximum_fusion = bf16[4,128,1280]{2,1,0:T(8,128)(2,1)} fusion(bf16[1,128,1280]{2,1,0:T(8,128)(2,1)} %bitcast.3, bf16[1,128,1280]{2,1,0:T(8,128)(2,1)} %bitcast.2, bf16[1,128,1280]{2,1,0:T(8,128)(2,1)} %bitcast.1, bf16[1,128,1280]{2,1,0:T(8,128)(2,1)S(1)} %fusion.29), kind=kLoop, calls=%fused_computation.13 | loop fusion | flops 1966080 | bytes 2621440 | tf_op jit(solution)/shard_map/stack | solution.py:30
  29.1 3.0 %gather_fusion = bf16[4,128,1280]{2,1,0:T(8,128)(2,1)} fusion(bf16[4,128,1280]{2,1,0:T(8,128)(2,1)} %pad_maximum_fusion, s32[1024]{0:T(1024)S(1)} %pad_clamp_fusion), kind=kCustom, calls=%fused_computation.clone | custom fusion | bytes 2621456 | tf_op jit(solution)/shard_map/jit(_take)/gather | solution.py:30
  32.2 1.6 broadcast_select_fusion.1
  33.8 0.3 copy-done.15
  34.1 2.4 %fusion.21 = (bf16[512,768]{1,0:T(8,128)(2,1)S(1)}, f32[512,768]{1,0:T(8,128)}) fusion(bf16[512,1280]{1,0:T(8,128)(2,1)S(1)} %bitcast.93, bf16[1280,768]{0,1:T(8,128)(2,1)S(1)} %bitcast.102), kind=kOutput, calls=%fused_computation.77 | convolution fusion | flops 1007026176 | bytes 5636096 | tf_op jit(solution)/shard_map/dot_general | solution.py:164
  36.5 0.1 fusion.19
  36.7 0.9 maximum_bitcast_fusion
  37.5 0.0 all-gather.4.cloned.1.call-update
  37.6 0.6 slice.106
  38.2 0.9 copy.19.qseg_ref
  39.1 0.6 pad.4
  39.7 2.3 %fusion.18 = (f32[512,64]{1,0:T(8,128)}, f32[512,64]{1,0:T(8,128)}, f32[512,64]{1,0:T(8,128)}, f32[512,64]{1,0:T(8,128)}) fusion(f32[512,768]{1,0:T(8,128)} %get-tuple-element.36), kind=kLoop, calls=%fused_computation.74 | loop fusion | bytes 1048576 | tf_op jit(solution)/shard_map/slice | solution.py:174
  42.0 2.4 %concatenate.16.proj_ref = f32[512,512]{1,0:T(8,128)} concatenate(f32[512,64]{1,0:T(8,128)} %get-tuple-element.18, f32[512,64]{1,0:T(8,128)S(1)} %broadcast.88, f32[512,64]{1,0:T(8,128)} %get-tuple-element.17, f32[512,64]{1,0:T(8,128)S(1)} %broadcast.88, f32[512,64]{1,0:T(8,128)} %get-tuple-element.16, f32[512,64]{1,0:T(8,128)S(1)} %broadcast.88, f32[512,64]{1,0:T(8,128)} %get-tuple-element.15, ...), dimensions={1} | concatenate | bytes 2097152 | tf_op jit(solution)/shard_map/concatenate | solution.py:170
  44.4 66.2 %all-gather.4.cloned.1.call-done.kv_ref = bf16[8,513,512]{2,1,0:T(8,128)(2,1)} async-done(((bf16[1,513,512]{2,1,0:T(8,128)(2,1)}), bf16[8,513,512]{2,1,0:T(8,128)(2,1)}) %all-gather.4.cloned.1.call-update) | async-done | bytes 4202512 | tf_op jit(solution)/shard_map/all_gather | solution.py:192
  110.6 0.8 slice.104
  111.5 0.6 copy.22
  112.1 1.3 convert_reduce_fusion
  113.5 1.3 pad_add_fusion.bounds_ref
  114.8 15.9 %shard_map.113 = bf16[512,256]{1,0:T(8,128)(2,1)} custom-call(s32[3]{0:T(128)} %pad_add_fusion.bounds_ref, f32[512,512]{1,0:T(8,128)} %concatenate.16.proj_ref, bf16[8,513,512]{2,1,0:T(8,128)(2,1)} %all-gather.4.cloned.1.call-done.kv_ref, f32[4,1,128]{2,1,0:T(1,128)} %bitcast.101, s32[512,1]{1,0:T(8,128)} %copy.19.qseg_ref, s32[1,4096]{1,0:T(1,128)} %bitcast.98), custom_call_target="tpu_custom_call" | custom-call | flops 4294967296 | bytes 4194304 | tf_op jit(solution)/shard_map/pallas_call | solution.py:128
  130.6 1.7 convolution_convert_fusion.1
  132.3 0.1 dynamic-slice_bitcast_fusion.5
  132.4 0.1 collective-permute-start.3
  132.5 1.5 collective-permute-start.4
  134.0 1.4 collective-permute-start.5
  135.4 0.2 select_reduce_fusion
  135.6 6.2 %collective-permute-done.3 = bf16[128,1280]{1,0:T(8,128)(2,1)S(1)} collective-permute-done((bf16[128,1280]{1,0:T(8,128)(2,1)S(1)}, bf16[128,1280]{1,0:T(8,128)(2,1)S(1)}, u32[]{:S(2)}, u32[]{:S(2)}) %collective-permute-start.3) | collective-permute-done | bytes 327712 | tf_op jit(solution)/shard_map/ppermute | solution.py:41
  141.9 1.2 collective-permute-done.4
  143.1 5.4 %collective-permute-done.5 = bf16[128,1280]{1,0:T(8,128)(2,1)S(1)} collective-permute-done((bf16[128,1280]{1,0:T(8,128)(2,1)S(1)}, bf16[128,1280]{1,0:T(8,128)(2,1)S(1)}, u32[]{:S(2)}, u32[]{:S(2)}) %collective-permute-start.5) | collective-permute-done | bytes 327712 | tf_op jit(solution)/shard_map/ppermute | solution.py:41
  148.5 0.3 multiply_reduce_fusion.3
  148.8 0.4 multiply_reduce_fusion.2
  149.2 0.1 multiply_convert_fusion.1
  149.3 0.9 collective-permute-start.6
  150.2 1.5 collective-permute-start.7
  151.7 0.1 fusion.28
  151.8 6.5 %collective-permute-done.6 = bf16[128,1280]{1,0:T(8,128)(2,1)S(1)} collective-permute-done((bf16[128,1280]{1,0:T(8,128)(2,1)S(1)}, bf16[128,1280]{1,0:T(8,128)(2,1)S(1)}, u32[]{:S(2)}, u32[]{:S(2)}) %collective-permute-start.6) | collective-permute-done | bytes 327712 | tf_op jit(solution)/shard_map/ppermute | solution.py:28
  158.3 2.6 %collective-permute-done.7 = bf16[128,1280]{1,0:T(8,128)(2,1)S(1)} collective-permute-done((bf16[128,1280]{1,0:T(8,128)(2,1)S(1)}, bf16[128,1280]{1,0:T(8,128)(2,1)S(1)}, u32[]{:S(2)}, u32[]{:S(2)}) %collective-permute-start.7) | collective-permute-done | bytes 327712 | tf_op jit(solution)/shard_map/ppermute | solution.py:28
  160.9 3.8 %collective-permute-done.8 = bf16[128,1280]{1,0:T(8,128)(2,1)S(1)} collective-permute-done((bf16[128,1280]{1,0:T(8,128)(2,1)S(1)}, bf16[128,1280]{1,0:T(8,128)(2,1)S(1)}, u32[]{:S(2)}, u32[]{:S(2)}) %collective-permute-start.8) | collective-permute-done | bytes 327712 | tf_op jit(solution)/shard_map/ppermute | solution.py:28
  164.7 1.2 pad_maximum_fusion.1
  165.9 3.2 %gather_fusion.1 = bf16[4,128,1280]{2,1,0:T(8,128)(2,1)} fusion(bf16[4,128,1280]{2,1,0:T(8,128)(2,1)} %pad_maximum_fusion.1, s32[1024]{0:T(1024)} %copy-done.9), kind=kCustom, calls=%fused_computation.1.clone | custom fusion | bytes 2621456 | tf_op jit(solution)/shard_map/jit(_take)/gather | solution.py:30
  169.1 1.5 broadcast_select_fusion
  170.6 6.3 %fusion = f32[512,2,1280]{2,0,1:T(8,128)S(1)} fusion(bf16[512,1280,1]{1,0,2:T(8,128)(2,1)S(1)} %bitcast.94, bf16[1280,2,1280]{2,1,0:T(2,128)(2,1)} %param.17), kind=kOutput, calls=%fused_computation.2 | convolution fusion | flops 3355443200 | bytes 13107200 | tf_op jit(solution)/shard_map/td,dkf->tkf/dot_general | solution.py:244
  177.0 2.5 %convolution_convert_fusion = bf16[512,1280]{1,0:T(8,128)(2,1)S(1)} fusion(bf16[1280,1280]{1,0:T(8,128)(2,1)S(1)} %copy-done, f32[512,2,1280]{2,0,1:T(8,128)S(1)} %fusion, f32[1280]{0:T(1024)S(1)} %get-tuple-element.6, f32[1280]{0:T(1024)S(1)} %get-tuple-element.5), kind=kOutput, calls=%fused_computation.4 | convolution fusion | flops 1684275200 | bytes 9840640 | tf_op jit(solution)/shard_map/dot_general | solution.py:250
  179.4 1.1 copy-done.4
  180.5 1.0 dynamic-slice_bitcast_fusion.2
  181.5 1.5 collective-permute-start.10
  183.0 1.6 collective-permute-start.11
  184.6 0.7 fusion.20
  195.7 1.4 constant_dynamic-slice_fusion.3
  197.1 0.9 pad_maximum_fusion.2
  197.9 0.3 collective-permute-done.11
  198.3 1.1 collective-permute-done.9
  199.4 1.4 multiply_reduce_fusion.1
  200.9 1.6 multiply_reduce_fusion
  202.5 0.9 multiply_convert_fusion
  (50 shorter events, 0.2 us)
Async XLA Ops:
  7.2 169.8 %copy-start = (bf16[1280,1280]{1,0:T(8,128)(2,1)S(1)}, bf16[1280,1280]{1,0:T(8,128)(2,1)}, u32[]{:S(2)}) copy-start(bf16[1280,1280]{1,0:T(8,128)(2,1)} %param.18) | copy-start | bytes 9830404
  7.2 103.4 %all-gather.4.cloned.1.call-start = ((), (), s32[]{:S(2)}) async-start(), calls=%async_computation | async-start | bytes 4792320 | tf_op jit(solution)/shard_map/all_gather | solution.py:192
  8.5 20.6 %copy-start.10 = (f32[128]{0:T(128)}, f32[128]{0:T(128)S(1)}, u32[]{:S(2)}) copy-start(f32[128]{0:T(128)S(1)} %add_rsqrt_fusion.4) | copy-start | bytes 1540
  10.3 9.8 %collective-permute-start = (bf16[128,1280]{1,0:T(8,128)(2,1)}, bf16[128,1280]{1,0:T(8,128)(2,1)}, u32[]{:S(2)}, u32[]{:S(2)}) collective-permute-start(bf16[128,1280]{1,0:T(8,128)(2,1)} %fusion.9), channel_id=1, source_target_pairs={{0,1},{1,2},{2,3},{3,0},{4,5},{5,6},{6,7},{7,4},{8,9},{9,10},{10,1... | collective-permute-start | bytes 983048 | tf_op jit(solution)/shard_map/ppermute | solution.py:28
  10.3 10.9 %collective-permute-start.1 = (bf16[128,1280]{1,0:T(8,128)(2,1)}, bf16[128,1280]{1,0:T(8,128)(2,1)}, u32[]{:S(2)}, u32[]{:S(2)}) collective-permute-start(bf16[128,1280]{1,0:T(8,128)(2,1)} %fusion.9), channel_id=1, source_target_pairs={{0,2},{1,3},{2,0},{3,1},{4,6},{5,7},{6,4},{7,5},{8,10},{9,11},{10,... | collective-permute-start | bytes 983048 | tf_op jit(solution)/shard_map/ppermute | solution.py:28
  11.9 14.8 %collective-permute-start.2 = (bf16[128,1280]{1,0:T(8,128)(2,1)}, bf16[128,1280]{1,0:T(8,128)(2,1)}, u32[]{:S(2)}, u32[]{:S(2)}) collective-permute-start(bf16[128,1280]{1,0:T(8,128)(2,1)} %fusion.9), channel_id=1, source_target_pairs={{0,3},{1,0},{2,1},{3,2},{4,7},{5,4},{6,5},{7,6},{8,11},{9,8},{10,9... | collective-permute-start | bytes 983048 | tf_op jit(solution)/shard_map/ppermute | solution.py:28
  13.3 18.8 %copy-start.13 = (pred[4]{0:T(512)(128)(4,1)}, pred[4]{0:T(512)(128)(4,1)S(1)}, u32[]{:S(2)}) copy-start(pred[4]{0:T(512)(128)(4,1)S(1)} %compare_and_fusion) | copy-start | bytes 16
  13.4 15.8 %copy-start.9 = (s32[1024]{0:T(1024)}, s32[1024]{0:T(1024)S(1)}, u32[]{:S(2)}) copy-start(s32[1024]{0:T(1024)S(1)} %pad_clamp_fusion) | copy-start | bytes 12292
  32.2 1.9 copy-start.15
  36.5 1.1 copy-start.8
  36.5 2.6 %copy-start.12 = (f32[4,64]{1,0:T(4,128)S(1)}, f32[4,64]{1,0:T(4,128)}, u32[]{:S(2)}) copy-start(f32[4,64]{1,0:T(4,128)} %param.19) | copy-start | bytes 3076
  36.5 3.1 %copy-start.6 = (f32[2,1280]{1,0:T(2,128)S(1)}, f32[2,1280]{1,0:T(2,128)}, u32[]{:S(2)}) copy-start(f32[2,1280]{1,0:T(2,128)} %param.21) | copy-start | bytes 30724
  132.3 3.1 %copy-start.7 = (f32[2,1280]{1,0:T(2,128)S(1)}, f32[2,1280]{1,0:T(2,128)}, u32[]{:S(2)}) copy-start(f32[2,1280]{1,0:T(2,128)} %param.20) | copy-start | bytes 30724
  132.3 3.1 %copy-start.16 = (s32[32]{0:T(128)S(1)}, s32[32]{0:T(128)}, u32[]{:S(2)}) copy-start(s32[32]{0:T(128)} %param.14) | copy-start | bytes 388
  132.3 16.5 %copy-start.3 = (bf16[128,1280]{1,0:T(8,128)(2,1)S(1)}, bf16[128,1280]{1,0:T(8,128)(2,1)}, u32[]{:S(2)}) copy-start(bf16[128,1280]{1,0:T(8,128)(2,1)} %param.12) | copy-start | bytes 983044
  132.3 16.5 %copy-start.11 = (f32[128]{0:T(128)S(1)}, f32[128]{0:T(128)}, u32[]{:S(2)}) copy-start(f32[128]{0:T(128)} %copy-done.10) | copy-start | bytes 1540
  132.4 9.5 %collective-permute-start.3 = (bf16[128,1280]{1,0:T(8,128)(2,1)S(1)}, bf16[128,1280]{1,0:T(8,128)(2,1)S(1)}, u32[]{:S(2)}, u32[]{:S(2)}) collective-permute-start(bf16[128,1280]{1,0:T(8,128)(2,1)S(1)} %get-tuple-element.22), channel_id=1, source_target_pairs={{0,1},{1,2},{2,3},{3,0},{4,5},{5,6},{6,7},{7,4},{8,9},{9,10},{10,1... | collective-permute-start | bytes 983048 | tf_op jit(solution)/shard_map/ppermute | solution.py:41
  132.5 10.6 %collective-permute-start.4 = (bf16[128,1280]{1,0:T(8,128)(2,1)S(1)}, bf16[128,1280]{1,0:T(8,128)(2,1)S(1)}, u32[]{:S(2)}, u32[]{:S(2)}) collective-permute-start(bf16[128,1280]{1,0:T(8,128)(2,1)S(1)} %get-tuple-element.24), channel_id=1, source_target_pairs={{0,2},{1,3},{2,0},{3,1},{4,6},{5,7},{6,4},{7,5},{8,10},{9,11},{10,... | collective-permute-start | bytes 983048 | tf_op jit(solution)/shard_map/ppermute | solution.py:41
  134.0 14.5 %collective-permute-start.5 = (bf16[128,1280]{1,0:T(8,128)(2,1)S(1)}, bf16[128,1280]{1,0:T(8,128)(2,1)S(1)}, u32[]{:S(2)}, u32[]{:S(2)}) collective-permute-start(bf16[128,1280]{1,0:T(8,128)(2,1)S(1)} %get-tuple-element.23), channel_id=1, source_target_pairs={{0,3},{1,0},{2,1},{3,2},{4,7},{5,4},{6,5},{7,6},{8,11},{9,8},{10,9... | collective-permute-start | bytes 983048 | tf_op jit(solution)/shard_map/ppermute | solution.py:41
  149.2 2.5 %copy-start.1 = (f32[128,1280]{1,0:T(8,128)}, f32[128,1280]{1,0:T(8,128)S(1)}, u32[]{:S(2)}) copy-start(f32[128,1280]{1,0:T(8,128)S(1)} %get-tuple-element.10) | copy-start | bytes 1966084
  149.3 8.9 %collective-permute-start.6 = (bf16[128,1280]{1,0:T(8,128)(2,1)S(1)}, bf16[128,1280]{1,0:T(8,128)(2,1)S(1)}, u32[]{:S(2)}, u32[]{:S(2)}) collective-permute-start(bf16[128,1280]{1,0:T(8,128)(2,1)S(1)} %multiply_convert_fusion.1), channel_id=1, source_target_pairs={{0,1},{1,2},{2,3},{3,0},{4,5},{5,6},{6,7},{7,4},{8,9},{9,10},{10,1... | collective-permute-start | bytes 983048 | tf_op jit(solution)/shard_map/ppermute | solution.py:28
  150.2 10.6 %collective-permute-start.7 = (bf16[128,1280]{1,0:T(8,128)(2,1)S(1)}, bf16[128,1280]{1,0:T(8,128)(2,1)S(1)}, u32[]{:S(2)}, u32[]{:S(2)}) collective-permute-start(bf16[128,1280]{1,0:T(8,128)(2,1)S(1)} %multiply_convert_fusion.1), channel_id=1, source_target_pairs={{0,2},{1,3},{2,0},{3,1},{4,6},{5,7},{6,4},{7,5},{8,10},{9,11},{10,... | collective-permute-start | bytes 983048 | tf_op jit(solution)/shard_map/ppermute | solution.py:28
  151.7 13.0 %collective-permute-start.8 = (bf16[128,1280]{1,0:T(8,128)(2,1)S(1)}, bf16[128,1280]{1,0:T(8,128)(2,1)S(1)}, u32[]{:S(2)}, u32[]{:S(2)}) collective-permute-start(bf16[128,1280]{1,0:T(8,128)(2,1)S(1)} %multiply_convert_fusion.1), channel_id=1, source_target_pairs={{0,3},{1,0},{2,1},{3,2},{4,7},{5,4},{6,5},{7,6},{8,11},{9,8},{10,9... | collective-permute-start | bytes 983048 | tf_op jit(solution)/shard_map/ppermute | solution.py:28
  165.9 3.2 %copy-start.14 = (pred[4]{0:T(512)(128)(4,1)S(1)}, pred[4]{0:T(512)(128)(4,1)}, u32[]{:S(2)}) copy-start(pred[4]{0:T(512)(128)(4,1)} %copy-done.13) | copy-start | bytes 16
  179.4 1.1 copy-start.4
  181.5 16.4 %collective-permute-start.10 = (bf16[128,1280]{1,0:T(8,128)(2,1)}, bf16[128,1280]{1,0:T(8,128)(2,1)}, u32[]{:S(2)}, u32[]{:S(2)}) collective-permute-start(bf16[128,1280]{1,0:T(8,128)(2,1)} %get-tuple-element.21), channel_id=1, source_target_pairs={{0,2},{1,3},{2,0},{3,1},{4,6},{5,7},{6,4},{7,5},{8,10},{9,11},{10,... | collective-permute-start | bytes 983048 | tf_op jit(solution)/shard_map/ppermute | solution.py:41
  183.0 15.3 %collective-permute-start.11 = (bf16[128,1280]{1,0:T(8,128)(2,1)}, bf16[128,1280]{1,0:T(8,128)(2,1)}, u32[]{:S(2)}, u32[]{:S(2)}) collective-permute-start(bf16[128,1280]{1,0:T(8,128)(2,1)} %get-tuple-element.20), channel_id=1, source_target_pairs={{0,3},{1,0},{2,1},{3,2},{4,7},{5,4},{6,5},{7,6},{8,11},{9,8},{10,9... | collective-permute-start | bytes 983048 | tf_op jit(solution)/shard_map/ppermute | solution.py:41
  184.6 14.8 %collective-permute-start.9 = (bf16[128,1280]{1,0:T(8,128)(2,1)}, bf16[128,1280]{1,0:T(8,128)(2,1)}, u32[]{:S(2)}, u32[]{:S(2)}) collective-permute-start(bf16[128,1280]{1,0:T(8,128)(2,1)} %get-tuple-element.19), channel_id=1, source_target_pairs={{0,1},{1,2},{2,3},{3,0},{4,5},{5,6},{6,7},{7,4},{8,9},{9,10},{10,1... | collective-permute-start | bytes 983048 | tf_op jit(solution)/shard_map/ppermute | solution.py:41
  195.7 3.7 %copy-start.5 = (bf16[512,1280]{1,0:T(8,128)(2,1)S(1)}, bf16[512,1280]{1,0:T(8,128)(2,1)}, u32[]{:S(2)}) copy-start(bf16[512,1280]{1,0:T(8,128)(2,1)} %copy-done.4) | copy-start | bytes 3932164
  197.1 3.8 %copy-start.2 = (f32[128,1280]{1,0:T(8,128)S(1)}, f32[128,1280]{1,0:T(8,128)}, u32[]{:S(2)}) copy-start(f32[128,1280]{1,0:T(8,128)} %copy-done.1) | copy-start | bytes 1966084
Sparse Core Ops, SparseCore 0:
  37.7 72.8 all-gather.3

commit v4 on v1

--- a/solution.py
+++ b/solution.py
@@ -59,6 +59,7 @@
     first = bounds_ref[2 * tiles]
     fold = factor == 2.0 ** round(math.log2(factor))
     key_lane = lax.broadcasted_iota(jnp.int32, (K_TILE, lanes), 1)
+    lane_pick = (lax.broadcasted_iota(jnp.int32, (lanes, lanes), 0) < half).astype(jnp.float32)
     held = {}
     for head in range(heads):
         scale = scale_ref[head]
@@ -83,10 +84,11 @@
                 key_at = pl.multiple_of(block * K_TILE, K_TILE)
                 kv_blk = kv_ref[shard, pl.ds(row_at, K_TILE), head * lanes : (head + 1) * lanes]
                 kv_f = kv_blk.astype(jnp.float32)
-                k_sq = jnp.where(key_lane < half, kv_f * kv_f, 0.0)
-                k_unit = (
-                    kv_f * lax.rsqrt(jnp.sum(k_sq, axis=1, keepdims=True) + EPSILON) * scale
-                ).astype(jnp.bfloat16)
+                k_sum = jnp.dot(
+                    kv_f * kv_f, lane_pick, precision=lax.Precision.HIGHEST,
+                    preferred_element_type=jnp.float32,
+                )
+                k_unit = (kv_f * lax.rsqrt(k_sum + EPSILON) * scale).astype(jnp.bfloat16)
                 k_seg = kseg_ref[:, pl.ds(key_at, K_TILE)]
                 scores = lax.dot_general(
                     q_tile, k_unit, (((1,), (1,)), ((), ())), preferred_element_type=jnp.float32

time: 210 us -> 213 us (1.014)
  the two profiles are of different devices: /device:TPU:10 before, /device:TPU:26 now
where the time goes in v4:
time: 213 us; the launch traced here: 212 us
  waiting for transfers between devices  105 us (49%)
  between operations  24.7 us (12%)
  local copies, waits for them, and re-layouts  21.6 us (10%)
  Pallas kernels  21 us (10%)
  matrix products  14.2 us (7%)
  other arithmetic  14 us (7%)
  starting transfers between devices  11.7 us (5%)
    all_gather x1, waiting for transfers between devices, body(): gathered = lax.all_gather(kv_ext, 'seq', axis=0, tiled=False)  67.5 us
    ppermute x6, waiting for transfers between devices, gather_rows(): came = lax.ppermute(part, axis, pairs)  22.3 us
    pallas_call x1, Pallas kernels, flash_attend(): pl.pallas_call(functools.partial(attend_kernel, factor=factor, half=half)...  21 us
    ppermute x6, waiting for transfers between devices, scatter_sum(): total = total + lax.ppermute(send, axis, pairs).astype(jnp.float32)  14.9 us
    reduce_sum x5, other arithmetic, unit_rows(): jnp.sum(matrix * matrix, axis=-1, keepdims=True) + EPSILON  7.59 us
    dot_general x1, matrix products, body(): jnp.einsum('td,dkf->tkf', mid_rows, up_proj, preferred_element_type=jnp.f...  6.36 us
    ppermute x6, starting transfers between devices, scatter_sum(): total = total + lax.ppermute(send, axis, pairs).astype(jnp.float32)  6.03 us
    ppermute x6, starting transfers between devices, gather_rows(): came = lax.ppermute(part, axis, pairs)  5.59 us
  transfers between devices with their start and end apart: 13, of which 11 were waited for; matrix products, arithmetic and copies ran while one was open for 6% of the time, Pallas kernels for 0%

profile of v4, /device:TPU:26, one launch (start us, length us, event | category | flops | bytes accessed | tf_op | source)
XLA Modules:
  0.0 211.9 jit_solution(11012424149290081082)
XLA Ops:
  7.2 0.0 copy-start
  7.2 0.0 all-gather.4.cloned.1.call-start
  7.2 1.3 fusion.9
  8.5 1.2 broadcast.73.clone
  9.7 0.9 constant_dynamic-update-slice_fusion.7
  10.7 1.6 collective-permute-start.1
  12.2 1.4 collective-permute-start.2
  13.7 6.7 %collective-permute-done = bf16[128,1280]{1,0:T(8,128)(2,1)} collective-permute-done((bf16[128,1280]{1,0:T(8,128)(2,1)}, bf16[128,1280]{1,0:T(8,128)(2,1)}, u32[]{:S(2)}, u32[]{:S(2)}) %collective-permute-start) | collective-permute-done | bytes 327712 | tf_op jit(solution)/shard_map/ppermute | solution.py:30
  20.4 1.7 constant_dynamic-update-slice_fusion.6
  22.1 1.7 constant_dynamic-update-slice_fusion.5
  23.9 3.2 %collective-permute-done.2 = bf16[128,1280]{1,0:T(8,128)(2,1)} collective-permute-done((bf16[128,1280]{1,0:T(8,128)(2,1)}, bf16[128,1280]{1,0:T(8,128)(2,1)}, u32[]{:S(2)}, u32[]{:S(2)}) %collective-permute-start.2) | collective-permute-done | bytes 327712 | tf_op jit(solution)/shard_map/ppermute | solution.py:30
  27.0 1.7 constant_dynamic-update-slice_fusion.4
  28.8 3.7 %fusion.22 = (bf16[512,768]{1,0:T(8,128)(2,1)S(1)}, f32[512,768]{1,0:T(8,128)}) fusion(bf16[512,1280]{1,0:T(8,128)(2,1)} %constant_dynamic-update-slice_fusion.4, bf16[1280,768]{0,1:T(8,128)(2,1)S(1)} %bitcast.85), kind=kOutput, calls=%fused_computation.73 | convolution fusion | flops 1007026176 | bytes 5636096 | tf_op jit(solution)/shard_map/dot_general | solution.py:168
  32.5 0.1 fusion.20
  32.6 0.9 maximum_bitcast_fusion
  33.5 0.0 all-gather.4.cloned.1.call-update
  33.6 0.6 slice.102
  34.1 0.9 copy.19.qseg_ref
  35.0 0.6 pad.4
  35.6 2.3 %fusion.19 = (f32[512,64]{1,0:T(8,128)}, f32[512,64]{1,0:T(8,128)}, f32[512,64]{1,0:T(8,128)}, f32[512,64]{1,0:T(8,128)}) fusion(f32[512,768]{1,0:T(8,128)} %get-tuple-element.39), kind=kLoop, calls=%fused_computation.70 | loop fusion | bytes 1048576 | tf_op jit(solution)/shard_map/slice | solution.py:178
  37.9 2.3 %concatenate.16.proj_ref = f32[512,512]{1,0:T(8,128)} concatenate(f32[512,64]{1,0:T(8,128)} %get-tuple-element.21, f32[512,64]{1,0:T(8,128)S(1)} %broadcast.74, f32[512,64]{1,0:T(8,128)} %get-tuple-element.20, f32[512,64]{1,0:T(8,128)S(1)} %broadcast.74, f32[512,64]{1,0:T(8,128)} %get-tuple-element.19, f32[512,64]{1,0:T(8,128)S(1)} %broadcast.74, f32[512,64]{1,0:T(8,128)} %get-tuple-element.18, ...), dimensions={1} | concatenate | bytes 2097152 | tf_op jit(solution)/shard_map/concatenate | solution.py:174
  40.3 67.5 %all-gather.4.cloned.1.call-done.kv_ref = bf16[8,513,512]{2,1,0:T(8,128)(2,1)} async-done(((bf16[1,513,512]{2,1,0:T(8,128)(2,1)}), bf16[8,513,512]{2,1,0:T(8,128)(2,1)}) %all-gather.4.cloned.1.call-update) | async-done | bytes 4202512 | tf_op jit(solution)/shard_map/all_gather | solution.py:196
  107.7 0.8 slice.100
  108.6 0.6 copy.22
  109.2 1.3 convert_reduce_fusion
  110.6 1.2 pad_add_fusion.bounds_ref
  111.8 21.0 %shard_map.113 = bf16[512,256]{1,0:T(8,128)(2,1)} custom-call(s32[3]{0:T(128)} %pad_add_fusion.bounds_ref, f32[512,512]{1,0:T(8,128)} %concatenate.16.proj_ref, bf16[8,513,512]{2,1,0:T(8,128)(2,1)} %all-gather.4.cloned.1.call-done.kv_ref, f32[4,1,128]{2,1,0:T(1,128)} %bitcast.84, s32[512,1]{1,0:T(8,128)} %copy.19.qseg_ref, s32[1,4096]{1,0:T(1,128)} %bitcast.81), custom_call_target="tpu_custom_call" | custom-call | flops 4294967296 | bytes 4194304 | tf_op jit(solution)/shard_map/pallas_call | solution.py:132
  132.8 1.7 convolution_convert_fusion.1
  134.5 0.0 copy-start.7
  134.5 1.1 copy-done.1
  135.6 1.0 dynamic-slice_bitcast_fusion.5
  136.6 1.5 collective-permute-start.4
  138.1 1.4 collective-permute-start.5
  139.6 6.8 %collective-permute-done.3 = bf16[128,1280]{1,0:T(8,128)(2,1)} collective-permute-done((bf16[128,1280]{1,0:T(8,128)(2,1)}, bf16[128,1280]{1,0:T(8,128)(2,1)}, u32[]{:S(2)}, u32[]{:S(2)}) %collective-permute-start.3) | collective-permute-done | bytes 327712 | tf_op jit(solution)/shard_map/ppermute | solution.py:43
  146.4 1.1 collective-permute-done.4
  147.5 5.5 %collective-permute-done.5 = bf16[128,1280]{1,0:T(8,128)(2,1)} collective-permute-done((bf16[128,1280]{1,0:T(8,128)(2,1)}, bf16[128,1280]{1,0:T(8,128)(2,1)}, u32[]{:S(2)}, u32[]{:S(2)}) %collective-permute-start.5) | collective-permute-done | bytes 327712 | tf_op jit(solution)/shard_map/ppermute | solution.py:43
  152.9 1.5 multiply_reduce_fusion.3
  154.5 1.8 multiply_reduce_fusion.2
  156.3 0.0 copy-start.12
  156.3 0.0 copy-start.8
  156.3 0.1 broadcast.73
  156.4 0.1 constant_dynamic-update-slice_fusion.3
  156.5 0.6 copy-done.2
  157.1 0.8 collective-permute-start.6
  157.9 0.2 select_reduce_fusion
  158.1 1.5 collective-permute-start.7
  159.7 0.2 collective-permute-start.8
  159.9 5.8 %collective-permute-done.6 = bf16[128,1280]{1,0:T(8,128)(2,1)S(1)} collective-permute-done((bf16[128,1280]{1,0:T(8,128)(2,1)S(1)}, bf16[128,1280]{1,0:T(8,128)(2,1)S(1)}, u32[]{:S(2)}, u32[]{:S(2)}) %collective-permute-start.6) | collective-permute-done | bytes 327712 | tf_op jit(solution)/shard_map/ppermute | solution.py:30
  165.7 3.1 %collective-permute-done.7 = bf16[128,1280]{1,0:T(8,128)(2,1)S(1)} collective-permute-done((bf16[128,1280]{1,0:T(8,128)(2,1)S(1)}, bf16[128,1280]{1,0:T(8,128)(2,1)S(1)}, u32[]{:S(2)}, u32[]{:S(2)}) %collective-permute-start.7) | collective-permute-done | bytes 327712 | tf_op jit(solution)/shard_map/ppermute | solution.py:30
  168.9 3.5 %collective-permute-done.8 = bf16[128,1280]{1,0:T(8,128)(2,1)S(1)} collective-permute-done((bf16[128,1280]{1,0:T(8,128)(2,1)S(1)}, bf16[128,1280]{1,0:T(8,128)(2,1)S(1)}, u32[]{:S(2)}, u32[]{:S(2)}) %collective-permute-start.8) | collective-permute-done | bytes 327712 | tf_op jit(solution)/shard_map/ppermute | solution.py:30
  172.4 6.4 %fusion = f32[512,2,1280]{2,0,1:T(8,128)S(1)} fusion(bf16[1280,2,1280]{2,1,0:T(2,128)(2,1)} %param.15, bf16[512,1280]{1,0:T(8,128)(2,1)S(1)} %constant_dynamic-update-slice_fusion), kind=kOutput, calls=%fused_computation | convolution fusion | flops 3355443200 | bytes 13107200 | tf_op jit(solution)/shard_map/td,dkf->tkf/dot_general | solution.py:248
  178.8 2.4 %convolution_convert_fusion = bf16[512,1280]{1,0:T(8,128)(2,1)S(1)} fusion(bf16[1280,1280]{1,0:T(8,128)(2,1)S(1)} %copy-done, f32[512,2,1280]{2,0,1:T(8,128)S(1)} %fusion, f32[1280]{0:T(1024)S(1)} %get-tuple-element.5, f32[1280]{0:T(1024)S(1)} %get-tuple-element.4), kind=kOutput, calls=%fused_computation.2 | convolution fusion | flops 1684275200 | bytes 9840640 | tf_op jit(solution)/shard_map/dot_general | solution.py:254
  181.2 1.1 copy-done.4
  182.3 1.0 dynamic-slice_bitcast_fusion.2
  183.3 1.5 collective-permute-start.10
  184.7 1.6 collective-permute-start.11
  186.4 0.7 fusion.21
  197.5 1.4 constant_dynamic-slice_fusion.3
  198.8 0.9 pad_maximum_fusion
  199.7 0.4 collective-permute-done.11
  200.0 1.1 collective-permute-done.9
  201.2 1.4 multiply_reduce_fusion.1
  202.7 1.6 multiply_reduce_fusion
  204.2 0.9 multiply_convert_fusion
  (39 shorter events, 0.3 us)
Async XLA Ops:
  7.2 171.6 %copy-start = (bf16[1280,1280]{1,0:T(8,128)(2,1)S(1)}, bf16[1280,1280]{1,0:T(8,128)(2,1)}, u32[]{:S(2)}) copy-start(bf16[1280,1280]{1,0:T(8,128)(2,1)} %param.16) | copy-start | bytes 9830404
  7.2 100.6 %all-gather.4.cloned.1.call-start = ((), (), s32[]{:S(2)}) async-start(), calls=%async_computation | async-start | bytes 4792320 | tf_op jit(solution)/shard_map/all_gather | solution.py:196
  7.2 6.4 %copy-start.9 = (s32[512]{0:T(512)S(1)}, s32[512]{0:T(512)}, u32[]{:S(2)}) copy-start(s32[512]{0:T(512)} %param.11) | copy-start | bytes 6148
  8.5 1.2 copy-start.6
  10.7 9.8 %collective-permute-start = (bf16[128,1280]{1,0:T(8,128)(2,1)}, bf16[128,1280]{1,0:T(8,128)(2,1)}, u32[]{:S(2)}, u32[]{:S(2)}) collective-permute-start(bf16[128,1280]{1,0:T(8,128)(2,1)} %get-tuple-element.13), channel_id=1, source_target_pairs={{0,1},{1,2},{2,3},{3,0},{4,5},{5,6},{6,7},{7,4},{8,9},{9,10},{10,1... | collective-permute-start | bytes 983048 | tf_op jit(solution)/shard_map/ppermute | solution.py:30
  10.7 11.5 %collective-permute-start.1 = (bf16[128,1280]{1,0:T(8,128)(2,1)}, bf16[128,1280]{1,0:T(8,128)(2,1)}, u32[]{:S(2)}, u32[]{:S(2)}) collective-permute-start(bf16[128,1280]{1,0:T(8,128)(2,1)} %get-tuple-element.13), channel_id=1, source_target_pairs={{0,2},{1,3},{2,0},{3,1},{4,6},{5,7},{6,4},{7,5},{8,10},{9,11},{10,... | collective-permute-start | bytes 983048 | tf_op jit(solution)/shard_map/ppermute | solution.py:30
  12.2 14.8 %collective-permute-start.2 = (bf16[128,1280]{1,0:T(8,128)(2,1)}, bf16[128,1280]{1,0:T(8,128)(2,1)}, u32[]{:S(2)}, u32[]{:S(2)}) collective-permute-start(bf16[128,1280]{1,0:T(8,128)(2,1)} %get-tuple-element.13), channel_id=1, source_target_pairs={{0,3},{1,0},{2,1},{3,2},{4,7},{5,4},{6,5},{7,6},{8,11},{9,8},{10,9... | collective-permute-start | bytes 983048 | tf_op jit(solution)/shard_map/ppermute | solution.py:30
  13.7 15.1 %copy-start.11 = (bf16[1280,4,192]{0,2,1:T(8,128)(2,1)S(1)}, bf16[1280,4,192]{0,2,1:T(8,128)(2,1)}, u32[]{:S(2)}) copy-start(bf16[1280,4,192]{0,2,1:T(8,128)(2,1)} %param.13) | copy-start | bytes 5898244
  32.5 2.5 %copy-start.10 = (f32[4,64]{1,0:T(4,128)S(1)}, f32[4,64]{1,0:T(4,128)}, u32[]{:S(2)}) copy-start(f32[4,64]{1,0:T(4,128)} %param.17) | copy-start | bytes 3076
  134.5 1.1 copy-start.1
  134.5 5.0 %copy-start.7 = (f32[2,1280]{1,0:T(2,128)S(1)}, f32[2,1280]{1,0:T(2,128)}, u32[]{:S(2)}) copy-start(f32[2,1280]{1,0:T(2,128)} %param.19) | copy-start | bytes 30724
  136.6 9.8 %collective-permute-start.3 = (bf16[128,1280]{1,0:T(8,128)(2,1)}, bf16[128,1280]{1,0:T(8,128)(2,1)}, u32[]{:S(2)}, u32[]{:S(2)}) collective-permute-start(bf16[128,1280]{1,0:T(8,128)(2,1)} %get-tuple-element.25), channel_id=1, source_target_pairs={{0,1},{1,2},{2,3},{3,0},{4,5},{5,6},{6,7},{7,4},{8,9},{9,10},{10,1... | collective-permute-start | bytes 983048 | tf_op jit(solution)/shard_map/ppermute | solution.py:43
  136.6 10.9 %collective-permute-start.4 = (bf16[128,1280]{1,0:T(8,128)(2,1)}, bf16[128,1280]{1,0:T(8,128)(2,1)}, u32[]{:S(2)}, u32[]{:S(2)}) collective-permute-start(bf16[128,1280]{1,0:T(8,128)(2,1)} %get-tuple-element.27), channel_id=1, source_target_pairs={{0,2},{1,3},{2,0},{3,1},{4,6},{5,7},{6,4},{7,5},{8,10},{9,11},{10,... | collective-permute-start | bytes 983048 | tf_op jit(solution)/shard_map/ppermute | solution.py:43
  138.1 14.8 %collective-permute-start.5 = (bf16[128,1280]{1,0:T(8,128)(2,1)}, bf16[128,1280]{1,0:T(8,128)(2,1)}, u32[]{:S(2)}, u32[]{:S(2)}) collective-permute-start(bf16[128,1280]{1,0:T(8,128)(2,1)} %get-tuple-element.26), channel_id=1, source_target_pairs={{0,3},{1,0},{2,1},{3,2},{4,7},{5,4},{6,5},{7,6},{8,11},{9,8},{10,9... | collective-permute-start | bytes 983048 | tf_op jit(solution)/shard_map/ppermute | solution.py:43
  156.2 0.8 copy-start.2
  156.3 1.7 copy-start.12
  156.3 3.4 %copy-start.8 = (f32[2,1280]{1,0:T(2,128)S(1)}, f32[2,1280]{1,0:T(2,128)}, u32[]{:S(2)}) copy-start(f32[2,1280]{1,0:T(2,128)} %param.18) | copy-start | bytes 30724
  157.1 8.6 %collective-permute-start.6 = (bf16[128,1280]{1,0:T(8,128)(2,1)S(1)}, bf16[128,1280]{1,0:T(8,128)(2,1)S(1)}, u32[]{:S(2)}, u32[]{:S(2)}) collective-permute-start(bf16[128,1280]{1,0:T(8,128)(2,1)S(1)} %get-tuple-element.9), channel_id=1, source_target_pairs={{0,1},{1,2},{2,3},{3,0},{4,5},{5,6},{6,7},{7,4},{8,9},{9,10},{10,1... | collective-permute-start | bytes 983048 | tf_op jit(solution)/shard_map/ppermute | solution.py:30
  158.1 10.7 %collective-permute-start.7 = (bf16[128,1280]{1,0:T(8,128)(2,1)S(1)}, bf16[128,1280]{1,0:T(8,128)(2,1)S(1)}, u32[]{:S(2)}, u32[]{:S(2)}) collective-permute-start(bf16[128,1280]{1,0:T(8,128)(2,1)S(1)} %get-tuple-element.9), channel_id=1, source_target_pairs={{0,2},{1,3},{2,0},{3,1},{4,6},{5,7},{6,4},{7,5},{8,10},{9,11},{10,... | collective-permute-start | bytes 983048 | tf_op jit(solution)/shard_map/ppermute | solution.py:30
  159.7 12.7 %collective-permute-start.8 = (bf16[128,1280]{1,0:T(8,128)(2,1)S(1)}, bf16[128,1280]{1,0:T(8,128)(2,1)S(1)}, u32[]{:S(2)}, u32[]{:S(2)}) collective-permute-start(bf16[128,1280]{1,0:T(8,128)(2,1)S(1)} %get-tuple-element.9), channel_id=1, source_target_pairs={{0,3},{1,0},{2,1},{3,2},{4,7},{5,4},{6,5},{7,6},{8,11},{9,8},{10,9... | collective-permute-start | bytes 983048 | tf_op jit(solution)/shard_map/ppermute | solution.py:30
  181.2 1.1 copy-start.4
  183.3 16.4 %collective-permute-start.10 = (bf16[128,1280]{1,0:T(8,128)(2,1)}, bf16[128,1280]{1,0:T(8,128)(2,1)}, u32[]{:S(2)}, u32[]{:S(2)}) collective-permute-start(bf16[128,1280]{1,0:T(8,128)(2,1)} %get-tuple-element.24), channel_id=1, source_target_pairs={{0,2},{1,3},{2,0},{3,1},{4,6},{5,7},{6,4},{7,5},{8,10},{9,11},{10,... | collective-permute-start | bytes 983048 | tf_op jit(solution)/shard_map/ppermute | solution.py:43
  184.7 15.3 %collective-permute-start.11 = (bf16[128,1280]{1,0:T(8,128)(2,1)}, bf16[128,1280]{1,0:T(8,128)(2,1)}, u32[]{:S(2)}, u32[]{:S(2)}) collective-permute-start(bf16[128,1280]{1,0:T(8,128)(2,1)} %get-tuple-element.23), channel_id=1, source_target_pairs={{0,3},{1,0},{2,1},{3,2},{4,7},{5,4},{6,5},{7,6},{8,11},{9,8},{10,9... | collective-permute-start | bytes 983048 | tf_op jit(solution)/shard_map/ppermute | solution.py:43
  186.4 14.8 %collective-permute-start.9 = (bf16[128,1280]{1,0:T(8,128)(2,1)}, bf16[128,1280]{1,0:T(8,128)(2,1)}, u32[]{:S(2)}, u32[]{:S(2)}) collective-permute-start(bf16[128,1280]{1,0:T(8,128)(2,1)} %get-tuple-element.22), channel_id=1, source_target_pairs={{0,1},{1,2},{2,3},{3,0},{4,5},{5,6},{6,7},{7,4},{8,9},{9,10},{10,1... | collective-permute-start | bytes 983048 | tf_op jit(solution)/shard_map/ppermute | solution.py:43
  197.4 3.7 %copy-start.5 = (bf16[512,1280]{1,0:T(8,128)(2,1)S(1)}, bf16[512,1280]{1,0:T(8,128)(2,1)}, u32[]{:S(2)}) copy-start(bf16[512,1280]{1,0:T(8,128)(2,1)} %copy-done.4) | copy-start | bytes 3932164
  198.8 3.8 %copy-start.3 = (f32[128,1280]{1,0:T(8,128)S(1)}, f32[128,1280]{1,0:T(8,128)}, u32[]{:S(2)}) copy-start(f32[128,1280]{1,0:T(8,128)} %copy-done.2) | copy-start | bytes 1966084
Sparse Core Ops, SparseCore 0:
  33.7 74.0 all-gather.3
